TPU v7x, 256 devices: a whole 4x4x8 slice. The times are simulated.
256 devices in a mesh: ctx: 32 (over y_hi, z, core), uly: 8 (over x, y_lo).
Axes of the slice: x: 4, y: 4 (y_hi: 2, y_lo: 2; y = y_hi * 2 + y_lo), z: 8, core: 2. Of those that a mesh axis runs over, the one named last changes fastest.
Arguments:
- queries: bfloat16 [32768, 4096], P(('ctx', 'uly')), may hold values from -200 to 200, as said below
- keys: bfloat16 [32768, 1024], P(('ctx', 'uly')), may hold values from -6 to 6, as said below
- values: bfloat16 [32768, 1024], P(('ctx', 'uly')), may hold values from -6 to 6
Outputs:
- attended: bfloat16 [32768, 4096], P(('ctx', 'uly'))
Inputs may be any that keep to these rules, and one draw needn't show every extreme that they name: `queries`: entries of order one, except that some query rows may be large. `keys`: entries of order one.
All inputs are finite; a program needn't handle non-finite values.
Results may differ from a plain program's by a relative error of at most 0.0055.
Values may be sent and summed in bfloat16 or wider, within the bound.
No kernel may reach another device: no remote copies, remote signals or barrier semaphores. Data moves between devices by JAX's collectives and lax.ppermute only.
A program may use at most 64 MiB of HBM per device.

v0:
```python
import jax
import jax.numpy as jnp
from jax import lax
from jax.sharding import PartitionSpec as P

HEAD_SIZE = 128
WINDOW_BLOCKS = 3


def passed_along(block, axis, distance):
    devices = range(lax.axis_size(axis))
    route = [(i - distance, i) for i in devices if i - distance in devices]
    return lax.ppermute(block, axis, route)


def on_device(queries, keys, values):
    scale_factor = HEAD_SIZE ** (-0.5)
    cycle_pos = lax.axis_index("ctx")
    query_here, key_here, value_here = (
        lax.all_to_all(queries, "uly", split_axis=1, concat_axis=0, tiled=True),
        lax.all_to_all(keys, "uly", split_axis=1, concat_axis=0, tiled=True),
        lax.all_to_all(values, "uly", split_axis=1, concat_axis=0, tiled=True),
    )
    block_len = query_here.shape[0]
    q_heads = query_here.shape[1] // HEAD_SIZE
    kv_heads = key_here.shape[1] // HEAD_SIZE
    group_size = q_heads // kv_heads
    row_block = min(block_len, 512)
    pieces = block_len // row_block
    item_count = q_heads * pieces
    query_items = (
        query_here.reshape(block_len, q_heads, HEAD_SIZE)
        .transpose(1, 0, 2)
        .reshape(item_count, row_block, HEAD_SIZE)
    )
    key_blocks = key_here.reshape(block_len, kv_heads, HEAD_SIZE).transpose(1, 0, 2)
    value_blocks = value_here.reshape(block_len, kv_heads, HEAD_SIZE).transpose(1, 0, 2)
    carry_state = (
        jnp.full((item_count, row_block), -1e30, jnp.float32),
        jnp.zeros((item_count, row_block), jnp.float32),
        jnp.zeros((item_count, row_block, HEAD_SIZE), jnp.float32),
    )

    def absorb(carry_state, key_set, value_set, step_back):

        def per_item(inputs):
            item_index, running_max, running_sum, weighted, query_rows = inputs
            key_value_index = item_index // (pieces * group_size)
            key_rows = lax.dynamic_index_in_dim(key_set, key_value_index, 0, keepdims=False)
            value_rows = lax.dynamic_index_in_dim(value_set, key_value_index, 0, keepdims=False)
            scores = (
                jnp.einsum("qd,td->qt", query_rows, key_rows, preferred_element_type=jnp.float32)
                * scale_factor
            )
            if step_back == 0:
                query_pos = item_index % pieces * row_block + jnp.arange(row_block, dtype=jnp.int32)
                key_pos = jnp.arange(block_len, dtype=jnp.int32)
                visible = key_pos[None, :] <= query_pos[:, None]
            else:
                visible = jnp.broadcast_to(cycle_pos >= step_back, scores.shape)
            scores = jnp.where(visible, scores, jnp.float32(-1e30))
            new_max = jnp.maximum(running_max, jnp.max(scores, axis=-1))
            weights = jnp.where(visible, jnp.exp(scores - new_max[:, None]), jnp.float32(0.0))
            factor = jnp.exp(running_max - new_max)
            new_sum = running_sum * factor + jnp.sum(weights, axis=-1)
            product = jnp.einsum(
                "qt,td->qd",
                weights.astype(jnp.bfloat16),
                value_rows,
                preferred_element_type=jnp.float32,
            )
            return (new_max, new_sum, weighted * factor[:, None] + product)

        return lax.map(
            per_item,
            (
                jnp.arange(item_count, dtype=jnp.int32),
                carry_state[0],
                carry_state[1],
                carry_state[2],
                query_items,
            ),
        )

    carry_state = absorb(carry_state, key_blocks, value_blocks, 0)
    current = (key_blocks, value_blocks)
    for step_back in range(1, WINDOW_BLOCKS + 1):
        current = passed_along((current[0], current[1]), "ctx", 1)
        carry_state = absorb(carry_state, current[0], current[1], step_back)
    output_rows = (carry_state[2] / carry_state[1][..., None]).astype(jnp.bfloat16)
    output_rows = (
        output_rows.reshape(q_heads, block_len, HEAD_SIZE)
        .transpose(1, 0, 2)
        .reshape(block_len, q_heads * HEAD_SIZE)
    )
    return lax.all_to_all(output_rows, "uly", split_axis=0, concat_axis=1, tiled=True)


def solution(mesh):
    placed = (P(("ctx", "uly"), None), P(("ctx", "uly"), None), P(("ctx", "uly"), None))
    return jax.shard_map(
        on_device, mesh=mesh, in_specs=placed, out_specs=P(("ctx", "uly"), None), check_vma=False
    )
```

profile of v0, /device:TPU:224, one launch (start us, length us, event | category | flops | bytes accessed | tf_op | source)
XLA Modules:
  0.0 230.6 jit_solution(9669332993076689675)
XLA Ops:
  1.7 5.3 %all-to-all-start.1 = ((bf16[128,8,128]{2,0,1:T(8,128)(2,1)}), bf16[128,8,128]{2,0,1:T(8,128)(2,1)S(1)}, u32[]{:S(2)}, u32[]{:S(2)}) async-start(bf16[128,8,128]{2,0,1:T(8,128)(2,1)} %copy_bitcast_fusion.1), calls=%async_computation.1 | async-start | bytes 524288 | tf_op jit(solution)/shard_map/all_to_all | solution.py:21
  7.0 1.7 copy_bitcast_fusion
  8.7 5.5 %all-to-all-done.1 = bf16[128,8,128]{2,0,1:T(8,128)(2,1)S(1)} async-done(((bf16[128,8,128]{2,0,1:T(8,128)(2,1)}), bf16[128,8,128]{2,0,1:T(8,128)(2,1)S(1)}, u32[]{:S(2)}, u32[]{:S(2)}) %all-to-all-start.1) | async-done | bytes 262176 | tf_op jit(solution)/shard_map/all_to_all | solution.py:21
  14.2 3.4 %all-to-all-start.2 = ((bf16[128,8,128]{2,0,1:T(8,128)(2,1)}), bf16[128,8,128]{2,0,1:T(8,128)(2,1)S(1)}, u32[]{:S(2)}, u32[]{:S(2)}) async-start(bf16[128,8,128]{2,0,1:T(8,128)(2,1)} %copy_bitcast_fusion), calls=%async_computation.2 | async-start | bytes 524288 | tf_op jit(solution)/shard_map/all_to_all | solution.py:22
  19.0 5.6 %all-to-all-done.2 = bf16[128,8,128]{2,0,1:T(8,128)(2,1)S(1)} async-done(((bf16[128,8,128]{2,0,1:T(8,128)(2,1)}), bf16[128,8,128]{2,0,1:T(8,128)(2,1)S(1)}, u32[]{:S(2)}, u32[]{:S(2)}) %all-to-all-start.2) | async-done | bytes 262176 | tf_op jit(solution)/shard_map/all_to_all | solution.py:22
  24.5 3.6 %all-to-all-start = ((bf16[128,8,512]{0,2,1:T(8,128)(2,1)}), bf16[128,8,512]{0,2,1:T(8,128)(2,1)S(1)}, u32[]{:S(2)}, u32[]{:S(2)}) async-start(bf16[128,8,512]{0,2,1:T(8,128)(2,1)} %bitcast.31), calls=%async_computation | async-start | bytes 2097152 | tf_op jit(solution)/shard_map/all_to_all | solution.py:20
  28.1 1.9 collective-permute-start
  30.0 1.9 collective-permute-start.1
  31.9 3.8 %collective-permute-done = bf16[1,1024,128]{2,1,0:T(8,128)(2,1)S(1)} collective-permute-done((bf16[1,1024,128]{2,1,0:T(8,128)(2,1)S(1)}, bf16[1,1024,128]{2,1,0:T(8,128)(2,1)S(1)}, u32[]{:S(2)}, u32[]{:S(2)}) %collective-permute-start) | collective-permute-done | bytes 262176 | tf_op jit(solution)/shard_map/ppermute | solution.py:13
  35.8 1.9 collective-permute-start.2
  38.6 5.5 %collective-permute-start.3 = (bf16[1,1024,128]{2,1,0:T(8,128)(2,1)S(1)}, bf16[1,1024,128]{2,1,0:T(8,128)(2,1)}, u32[]{:S(2)}, u32[]{:S(2)}) collective-permute-start(bf16[1,1024,128]{2,1,0:T(8,128)(2,1)S(1)} %collective-permute-done.1), channel_id=1, source_target_pairs={{0,8},{8,16},{16,24},{24,32},{32,40},{40,48},{48,56},{56,64},{64,7... | collective-permute-start | bytes 786440 | tf_op jit(solution)/shard_map/ppermute | solution.py:13
  44.1 3.2 %collective-permute-start.4 = (bf16[1,1024,128]{2,1,0:T(8,128)(2,1)}, bf16[1,1024,128]{2,1,0:T(8,128)(2,1)S(1)}, u32[]{:S(2)}, u32[]{:S(2)}) collective-permute-start(bf16[1,1024,128]{2,1,0:T(8,128)(2,1)} %collective-permute-done.2), channel_id=1, source_target_pairs={{0,8},{8,16},{16,24},{24,32},{32,40},{40,48},{48,56},{56,64},{64,7... | collective-permute-start | bytes 786440 | tf_op jit(solution)/shard_map/ppermute | solution.py:13
  47.4 8.1 %collective-permute-start.5 = (bf16[1,1024,128]{2,1,0:T(8,128)(2,1)}, bf16[1,1024,128]{2,1,0:T(8,128)(2,1)}, u32[]{:S(2)}, u32[]{:S(2)}) collective-permute-start(bf16[1,1024,128]{2,1,0:T(8,128)(2,1)} %collective-permute-done.3), channel_id=1, source_target_pairs={{0,8},{8,16},{16,24},{24,32},{32,40},{40,48},{48,56},{56,64},{64,7... | collective-permute-start | bytes 786440 | tf_op jit(solution)/shard_map/ppermute | solution.py:13
  57.5 1.6 copy.19
  59.1 1.5 broadcast.122.clone.2
  60.6 44.1 %while.65 = (s32[]{:T(128)}, f32[8,512]{1,0:T(8,128)S(1)}, f32[8,512]{1,0:T(8,128)S(1)}, f32[8,512,128]{2,1,0:T(8,128)}, s32[8]{0:T(128)S(1)}, /*index=5*/bf16[8...) while((s32[]{:T(128)}, f32[8,512]{1,0:T(8,128)S(1)}, ...), condition=%wide.region_3.4_spmd, body=%wide.region_0.3_spmd.sunk | while | flops 276892160 | bytes 7248650 | solution.py:74
  69.2 1.5 fusion.106
  80.3 1.5 fusion.106
  104.7 1.5 broadcast.122.clone.1
  106.3 28.9 %while.66 = (s32[]{:T(128)}, f32[8,512]{1,0:T(8,128)S(1)}, f32[8,512]{1,0:T(8,128)S(1)}, f32[8,512,128]{2,1,0:T(8,128)}, f32[8,512]{1,0:T(8,128)S(1)}, /*index=5...) while((s32[]{:T(128)}, f32[8,512]{1,0:T(8,128)S(1)}, ...), condition=%wide.region_7.8_spmd, body=%wide.region_4.7_spmd.sunk | while | flops 275384320 | bytes 7515283 | solution.py:74
  106.8 2.3 fusion.111
  110.4 2.3 fusion.111
  114.1 2.3 fusion.111
  117.7 2.2 fusion.111
  121.3 2.3 fusion.111
  124.9 2.2 fusion.111
  128.5 2.2 fusion.111
  132.1 2.3 fusion.111
  135.1 1.5 broadcast.122.clone
  136.6 37.1 %while.67 = (s32[]{:T(128)}, f32[8,512]{1,0:T(8,128)S(1)}, f32[8,512]{1,0:T(8,128)S(1)}, f32[8,512,128]{2,1,0:T(8,128)}, f32[8,512]{1,0:T(8,128)S(1)}, /*index=5...) while((s32[]{:T(128)}, f32[8,512]{1,0:T(8,128)S(1)}, ...), condition=%wide.region_11.12_spmd, body=%wide.region_8.11_spmd.sunk | while | flops 275384320 | bytes 7515283 | solution.py:74
  136.6 1.5 fusion.114
  138.1 2.3 %fusion.116 = f32[8,512,128]{2,1,0:T(8,128)} fusion(f32[8,512,128]{2,1,0:T(8,128)} %get-tuple-element.1046, s32[]{:T(128)} %get-tuple-element.1043, f32[512,1024]{1,0:T(8,128)S(1)} %get-tuple-element.935, f32[512]{0:T(512)S(1)} %get-tuple-element.937, pred[]{:T(512)} %get-tuple-element.1061, bf16[1,1024,128]{2,1,0:T(8,128)(2,1)} %get-tuple-element.1066, ...), kind=kOutput, calls=%fused_computation.58.clone.1 | convolution fusion | flops 136970240 | bytes 2888704 | tf_op jit(solution)/shard_map/while/body/eval_jaxpr/qt,td->qd/dot_general | solution.py:66
  141.3 1.5 fusion.114
  142.8 2.3 %fusion.116 = f32[8,512,128]{2,1,0:T(8,128)} fusion(f32[8,512,128]{2,1,0:T(8,128)} %get-tuple-element.1046, s32[]{:T(128)} %get-tuple-element.1043, f32[512,1024]{1,0:T(8,128)S(1)} %get-tuple-element.935, f32[512]{0:T(512)S(1)} %get-tuple-element.937, pred[]{:T(512)} %get-tuple-element.1061, bf16[1,1024,128]{2,1,0:T(8,128)(2,1)} %get-tuple-element.1066, ...), kind=kOutput, calls=%fused_computation.58.clone.1 | convolution fusion | flops 136970240 | bytes 2888704 | tf_op jit(solution)/shard_map/while/body/eval_jaxpr/qt,td->qd/dot_general | solution.py:66
  145.9 1.5 fusion.114
  147.4 2.3 %fusion.116 = f32[8,512,128]{2,1,0:T(8,128)} fusion(f32[8,512,128]{2,1,0:T(8,128)} %get-tuple-element.1046, s32[]{:T(128)} %get-tuple-element.1043, f32[512,1024]{1,0:T(8,128)S(1)} %get-tuple-element.935, f32[512]{0:T(512)S(1)} %get-tuple-element.937, pred[]{:T(512)} %get-tuple-element.1061, bf16[1,1024,128]{2,1,0:T(8,128)(2,1)} %get-tuple-element.1066, ...), kind=kOutput, calls=%fused_computation.58.clone.1 | convolution fusion | flops 136970240 | bytes 2888704 | tf_op jit(solution)/shard_map/while/body/eval_jaxpr/qt,td->qd/dot_general | solution.py:66
  150.6 1.5 fusion.114
  152.1 2.4 %fusion.116 = f32[8,512,128]{2,1,0:T(8,128)} fusion(f32[8,512,128]{2,1,0:T(8,128)} %get-tuple-element.1046, s32[]{:T(128)} %get-tuple-element.1043, f32[512,1024]{1,0:T(8,128)S(1)} %get-tuple-element.935, f32[512]{0:T(512)S(1)} %get-tuple-element.937, pred[]{:T(512)} %get-tuple-element.1061, bf16[1,1024,128]{2,1,0:T(8,128)(2,1)} %get-tuple-element.1066, ...), kind=kOutput, calls=%fused_computation.58.clone.1 | convolution fusion | flops 136970240 | bytes 2888704 | tf_op jit(solution)/shard_map/while/body/eval_jaxpr/qt,td->qd/dot_general | solution.py:66
  155.2 1.5 fusion.114
  156.7 2.3 %fusion.116 = f32[8,512,128]{2,1,0:T(8,128)} fusion(f32[8,512,128]{2,1,0:T(8,128)} %get-tuple-element.1046, s32[]{:T(128)} %get-tuple-element.1043, f32[512,1024]{1,0:T(8,128)S(1)} %get-tuple-element.935, f32[512]{0:T(512)S(1)} %get-tuple-element.937, pred[]{:T(512)} %get-tuple-element.1061, bf16[1,1024,128]{2,1,0:T(8,128)(2,1)} %get-tuple-element.1066, ...), kind=kOutput, calls=%fused_computation.58.clone.1 | convolution fusion | flops 136970240 | bytes 2888704 | tf_op jit(solution)/shard_map/while/body/eval_jaxpr/qt,td->qd/dot_general | solution.py:66
  159.9 1.5 fusion.114
  161.4 2.3 %fusion.116 = f32[8,512,128]{2,1,0:T(8,128)} fusion(f32[8,512,128]{2,1,0:T(8,128)} %get-tuple-element.1046, s32[]{:T(128)} %get-tuple-element.1043, f32[512,1024]{1,0:T(8,128)S(1)} %get-tuple-element.935, f32[512]{0:T(512)S(1)} %get-tuple-element.937, pred[]{:T(512)} %get-tuple-element.1061, bf16[1,1024,128]{2,1,0:T(8,128)(2,1)} %get-tuple-element.1066, ...), kind=kOutput, calls=%fused_computation.58.clone.1 | convolution fusion | flops 136970240 | bytes 2888704 | tf_op jit(solution)/shard_map/while/body/eval_jaxpr/qt,td->qd/dot_general | solution.py:66
  164.5 1.5 fusion.114
  166.0 2.3 %fusion.116 = f32[8,512,128]{2,1,0:T(8,128)} fusion(f32[8,512,128]{2,1,0:T(8,128)} %get-tuple-element.1046, s32[]{:T(128)} %get-tuple-element.1043, f32[512,1024]{1,0:T(8,128)S(1)} %get-tuple-element.935, f32[512]{0:T(512)S(1)} %get-tuple-element.937, pred[]{:T(512)} %get-tuple-element.1061, bf16[1,1024,128]{2,1,0:T(8,128)(2,1)} %get-tuple-element.1066, ...), kind=kOutput, calls=%fused_computation.58.clone.1 | convolution fusion | flops 136970240 | bytes 2888704 | tf_op jit(solution)/shard_map/while/body/eval_jaxpr/qt,td->qd/dot_general | solution.py:66
  169.2 1.5 fusion.114
  170.7 2.3 %fusion.116 = f32[8,512,128]{2,1,0:T(8,128)} fusion(f32[8,512,128]{2,1,0:T(8,128)} %get-tuple-element.1046, s32[]{:T(128)} %get-tuple-element.1043, f32[512,1024]{1,0:T(8,128)S(1)} %get-tuple-element.935, f32[512]{0:T(512)S(1)} %get-tuple-element.937, pred[]{:T(512)} %get-tuple-element.1061, bf16[1,1024,128]{2,1,0:T(8,128)(2,1)} %get-tuple-element.1066, ...), kind=kOutput, calls=%fused_computation.58.clone.1 | convolution fusion | flops 136970240 | bytes 2888704 | tf_op jit(solution)/shard_map/while/body/eval_jaxpr/qt,td->qd/dot_general | solution.py:66
  174.6 31.1 %while.68 = (s32[]{:T(128)}, f32[8,512]{1,0:T(8,128)S(1)}, f32[8,512,128]{2,1,0:T(8,128)S(1)}, f32[8,512]{1,0:T(8,128)S(1)}, f32[8,512]{1,0:T(8,128)S(1)}, /*ind...) while((s32[]{:T(128)}, f32[8,512]{1,0:T(8,128)S(1)}, ...), condition=%wide.region_15.16_spmd, body=%wide.region_12.15_spmd.sunk | while | flops 275384320 | bytes 7508108 | solution.py:74
  174.7 1.5 fusion.119
  176.2 1.6 fusion.122
  178.5 1.5 fusion.119
  180.1 1.6 fusion.122
  182.4 1.5 fusion.119
  183.9 1.6 fusion.122
  186.3 1.5 fusion.119
  187.8 1.6 fusion.122
  190.2 1.5 fusion.119
  191.7 1.6 fusion.122
  194.1 1.5 fusion.119
  195.6 1.6 fusion.122
  198.0 1.5 fusion.119
  199.5 1.6 fusion.122
  201.9 1.5 fusion.119
  203.4 1.6 fusion.122
  207.4 21.8 %all_to_all.67 = bf16[8,128,512]{1,2,0:T(8,128)(2,1)S(1)} all-to-all(bf16[8,128,512]{1,2,0:T(8,128)(2,1)S(1)} %copy.23), channel_id=1, replica_groups=mesh['ctx'=32,'uly'=8] {'uly'}, dimensions={0} | all-to-all | bytes 2097152 | tf_op jit(solution)/shard_map/all_to_all | solution.py:96
  (248 shorter events, 57.5 us)
Async XLA Ops:
  0.0 1.0 copy-start
  1.0 16.7 %copy-start.2 = (bf16[128,4096]{1,0:T(8,128)(2,1)S(1)}, bf16[128,4096]{1,0:T(8,128)(2,1)}, u32[]{:S(2)}) copy-start(bf16[128,4096]{1,0:T(8,128)(2,1)} %param.11) | copy-start | bytes 3145732
  1.7 12.5 %all-to-all-start.1 = ((bf16[128,8,128]{2,0,1:T(8,128)(2,1)}), bf16[128,8,128]{2,0,1:T(8,128)(2,1)S(1)}, u32[]{:S(2)}, u32[]{:S(2)}) async-start(bf16[128,8,128]{2,0,1:T(8,128)(2,1)} %copy_bitcast_fusion.1), calls=%async_computation.1 | async-start | bytes 524288 | tf_op jit(solution)/shard_map/all_to_all | solution.py:21
  14.2 10.3 %all-to-all-start.2 = ((bf16[128,8,128]{2,0,1:T(8,128)(2,1)}), bf16[128,8,128]{2,0,1:T(8,128)(2,1)S(1)}, u32[]{:S(2)}, u32[]{:S(2)}) async-start(bf16[128,8,128]{2,0,1:T(8,128)(2,1)} %copy_bitcast_fusion), calls=%async_computation.2 | async-start | bytes 524288 | tf_op jit(solution)/shard_map/all_to_all | solution.py:22
  24.5 31.0 %all-to-all-start = ((bf16[128,8,512]{0,2,1:T(8,128)(2,1)}), bf16[128,8,512]{0,2,1:T(8,128)(2,1)S(1)}, u32[]{:S(2)}, u32[]{:S(2)}) async-start(bf16[128,8,512]{0,2,1:T(8,128)(2,1)} %bitcast.31), calls=%async_computation | async-start | bytes 2097152 | tf_op jit(solution)/shard_map/all_to_all | solution.py:20
  28.1 7.7 %collective-permute-start = (bf16[1,1024,128]{2,1,0:T(8,128)(2,1)S(1)}, bf16[1,1024,128]{2,1,0:T(8,128)(2,1)S(1)}, u32[]{:S(2)}, u32[]{:S(2)}) collective-permute-start(bf16[1,1024,128]{2,1,0:T(8,128)(2,1)S(1)} %bitcast.198), channel_id=1, source_target_pairs={{0,8},{8,16},{16,24},{24,32},{32,40},{40,48},{48,56},{56,64},{64,7... | collective-permute-start | bytes 786440 | tf_op jit(solution)/shard_map/ppermute | solution.py:13
  30.0 8.6 %collective-permute-start.1 = (bf16[1,1024,128]{2,1,0:T(8,128)(2,1)S(1)}, bf16[1,1024,128]{2,1,0:T(8,128)(2,1)S(1)}, u32[]{:S(2)}, u32[]{:S(2)}) collective-permute-start(bf16[1,1024,128]{2,1,0:T(8,128)(2,1)S(1)} %bitcast.200), channel_id=1, source_target_pairs={{0,8},{8,16},{16,24},{24,32},{32,40},{40,48},{48,56},{56,64},{64,7... | collective-permute-start | bytes 786440 | tf_op jit(solution)/shard_map/ppermute | solution.py:13
  35.8 8.3 %collective-permute-start.2 = (bf16[1,1024,128]{2,1,0:T(8,128)(2,1)S(1)}, bf16[1,1024,128]{2,1,0:T(8,128)(2,1)}, u32[]{:S(2)}, u32[]{:S(2)}) collective-permute-start(bf16[1,1024,128]{2,1,0:T(8,128)(2,1)S(1)} %collective-permute-done), channel_id=1, source_target_pairs={{0,8},{8,16},{16,24},{24,32},{32,40},{40,48},{48,56},{56,64},{64,7... | collective-permute-start | bytes 786440 | tf_op jit(solution)/shard_map/ppermute | solution.py:13
  38.6 16.9 %copy-start.3 = (bf16[1,1024,128]{2,1,0:T(8,128)(2,1)}, bf16[1,1024,128]{2,1,0:T(8,128)(2,1)S(1)}, u32[]{:S(2)}) copy-start(bf16[1,1024,128]{2,1,0:T(8,128)(2,1)S(1)} %collective-permute-done.1) | copy-start | bytes 786436
  38.6 8.8 %collective-permute-start.3 = (bf16[1,1024,128]{2,1,0:T(8,128)(2,1)S(1)}, bf16[1,1024,128]{2,1,0:T(8,128)(2,1)}, u32[]{:S(2)}, u32[]{:S(2)}) collective-permute-start(bf16[1,1024,128]{2,1,0:T(8,128)(2,1)S(1)} %collective-permute-done.1), channel_id=1, source_target_pairs={{0,8},{8,16},{16,24},{24,32},{32,40},{40,48},{48,56},{56,64},{64,7... | collective-permute-start | bytes 786440 | tf_op jit(solution)/shard_map/ppermute | solution.py:13
  44.1 129.7 %collective-permute-start.4 = (bf16[1,1024,128]{2,1,0:T(8,128)(2,1)}, bf16[1,1024,128]{2,1,0:T(8,128)(2,1)S(1)}, u32[]{:S(2)}, u32[]{:S(2)}) collective-permute-start(bf16[1,1024,128]{2,1,0:T(8,128)(2,1)} %collective-permute-done.2), channel_id=1, source_target_pairs={{0,8},{8,16},{16,24},{24,32},{32,40},{40,48},{48,56},{56,64},{64,7... | collective-permute-start | bytes 786440 | tf_op jit(solution)/shard_map/ppermute | solution.py:13
  47.4 126.4 %collective-permute-start.5 = (bf16[1,1024,128]{2,1,0:T(8,128)(2,1)}, bf16[1,1024,128]{2,1,0:T(8,128)(2,1)}, u32[]{:S(2)}, u32[]{:S(2)}) collective-permute-start(bf16[1,1024,128]{2,1,0:T(8,128)(2,1)} %collective-permute-done.3), channel_id=1, source_target_pairs={{0,8},{8,16},{16,24},{24,32},{32,40},{40,48},{48,56},{56,64},{64,7... | collective-permute-start | bytes 786440 | tf_op jit(solution)/shard_map/ppermute | solution.py:13
  104.7 1.5 copy-start.4
  173.8 0.7 copy-start.1
where the time goes:
time: 232 us; the launch traced here: 231 us
  matrix products  93.9 us (40%)
  starting transfers between devices  34.9 us (15%)
  local copies, waits for them, and re-layouts  24.1 us (10%)
  other arithmetic  22.6 us (10%)
  blocking collectives  21.8 us (9%)
  loops' own time  17.1 us (7%)
  waiting for transfers between devices  15.8 us (7%)
    dot_general x32, matrix products, per_item(): jnp.einsum('qt,td->qd', weights.astype(jnp.bfloat16), value_rows, preferr...  61.3 us
    dot_general x32, matrix products, per_item(): jnp.einsum('qd,td->qt', query_rows, key_rows, preferred_element_type=jnp....  32.6 us
    ppermute x6, starting transfers between devices, passed_along(): return lax.ppermute(block, axis, route)  22.6 us
    all_to_all x1, blocking collectives, on_device(): lax.all_to_all(output_rows, 'uly', split_axis=0, concat_axis=1, tiled=True)  21.8 us
    reduce_sum x32, other arithmetic, per_item(): new_sum = running_sum * factor + jnp.sum(weights, axis=-1)  21.1 us
    another operation x4, loops' own time, absorb(): lax.map(per_item, (jnp.arange(item_count, dtype=jnp.int32), carry_state[0...  17.1 us
    all_to_all x1, waiting for transfers between devices, on_device(): lax.all_to_all(values, 'uly', split_axis=1, concat_axis=0, tiled=True)  5.55 us
    all_to_all x1, waiting for transfers between devices, on_device(): lax.all_to_all(keys, 'uly', split_axis=1, concat_axis=0, tiled=True)  5.52 us
  transfers between devices with their start and end apart: 9, of which 4 were waited for; matrix products, arithmetic and copies ran while one was open for 45% of the time, Pallas kernels for 0%

commit v1 on v0

v1 whole, which is shorter than its diff:
```python
import functools

import jax
import jax.numpy as jnp
from jax import lax
from jax.experimental import pallas as pl
from jax.experimental.pallas import tpu as pltpu
from jax.sharding import PartitionSpec as P

HEAD_SIZE = 128
WINDOW_BLOCKS = 3
TILE = 512


def passed_along(block, axis, distance):
    devices = range(lax.axis_size(axis))
    route = [(i - distance, i) for i in devices if i - distance in devices]
    return lax.ppermute(block, axis, route)


def attend_kernel(pos_ref, q_ref, k_ref, v_ref, o_ref, m_ref, l_ref, acc_ref, *, block_len):
    i = pl.program_id(1)
    cycle_pos = pos_ref[0]
    scale_factor = HEAD_SIZE ** (-0.5)
    q = q_ref[...]
    m_ref[...] = jnp.full(m_ref.shape, -jnp.inf, jnp.float32)
    l_ref[...] = jnp.zeros(l_ref.shape, jnp.float32)
    acc_ref[...] = jnp.zeros(acc_ref.shape, jnp.float32)

    def process(start, masked):
        k = k_ref[pl.ds(start, TILE), :]
        v = v_ref[pl.ds(start, TILE), :]
        s = lax.dot_general(q, k, (((1,), (1,)), ((), ())), preferred_element_type=jnp.float32)
        s = s * scale_factor
        if masked:
            rows = lax.broadcasted_iota(jnp.int32, s.shape, 0)
            cols = lax.broadcasted_iota(jnp.int32, s.shape, 1)
            s = jnp.where(cols <= rows, s, jnp.float32(-1e30))
        m_old = m_ref[...]
        m_new = jnp.maximum(m_old, jnp.max(s, axis=-1, keepdims=True))
        p = jnp.exp(s - m_new)
        factor = jnp.exp(m_old - m_new)
        l_ref[...] = l_ref[...] * factor + jnp.sum(p, axis=-1, keepdims=True)
        pv = jnp.dot(p.astype(jnp.bfloat16), v, preferred_element_type=jnp.float32)
        acc_ref[...] = acc_ref[...] * factor + pv
        m_ref[...] = m_new

    diag = WINDOW_BLOCKS * block_len
    process(pl.multiple_of(diag + i * TILE, TILE), True)
    tiles = block_len // TILE
    for t in range(tiles - 1):
        @pl.when(i > t)
        def _():
            process(diag + t * TILE, False)

    for back in range(1, WINDOW_BLOCKS + 1):
        base = (WINDOW_BLOCKS - back) * block_len

        @pl.when(cycle_pos >= back)
        def _():
            for t in range(tiles):
                process(base + t * TILE, False)

    o_ref[...] = (acc_ref[...] / l_ref[...]).astype(o_ref.dtype)


def attend(cycle_pos, query_here, key_all, value_all):
    block_len, width = query_here.shape
    q_heads = width // HEAD_SIZE
    window = key_all.shape[0]
    kernel = functools.partial(attend_kernel, block_len=block_len)
    grid_spec = pltpu.PrefetchScalarGridSpec(
        num_scalar_prefetch=1,
        grid=(q_heads, block_len // TILE),
        in_specs=[
            pl.BlockSpec((TILE, HEAD_SIZE), lambda h, i, pos: (i, h)),
            pl.BlockSpec((window, HEAD_SIZE), lambda h, i, pos: (0, 0)),
            pl.BlockSpec((window, HEAD_SIZE), lambda h, i, pos: (0, 0)),
        ],
        out_specs=pl.BlockSpec((TILE, HEAD_SIZE), lambda h, i, pos: (i, h)),
        scratch_shapes=[
            pltpu.VMEM((TILE, 1), jnp.float32),
            pltpu.VMEM((TILE, 1), jnp.float32),
            pltpu.VMEM((TILE, HEAD_SIZE), jnp.float32),
        ],
    )
    return pl.pallas_call(
        kernel,
        grid_spec=grid_spec,
        out_shape=jax.ShapeDtypeStruct((block_len, width), jnp.bfloat16),
        compiler_params=pltpu.CompilerParams(dimension_semantics=("arbitrary", "arbitrary")),
    )(cycle_pos, query_here, key_all, value_all)


def on_device(queries, keys, values):
    cycle_pos = lax.axis_index("ctx")
    query_here, key_here, value_here = (
        lax.all_to_all(queries, "uly", split_axis=1, concat_axis=0, tiled=True),
        lax.all_to_all(keys, "uly", split_axis=1, concat_axis=0, tiled=True),
        lax.all_to_all(values, "uly", split_axis=1, concat_axis=0, tiled=True),
    )
    key_list = [key_here]
    value_list = [value_here]
    current = (key_here, value_here)
    for step_back in range(1, WINDOW_BLOCKS + 1):
        current = passed_along((current[0], current[1]), "ctx", 1)
        key_list.insert(0, current[0])
        value_list.insert(0, current[1])
    key_all = jnp.concatenate(key_list, axis=0)
    value_all = jnp.concatenate(value_list, axis=0)
    pos = jnp.reshape(cycle_pos, (1,)).astype(jnp.int32)
    output_rows = attend(pos, query_here, key_all, value_all)
    return lax.all_to_all(output_rows, "uly", split_axis=0, concat_axis=1, tiled=True)


def solution(mesh):
    placed = (P(("ctx", "uly"), None), P(("ctx", "uly"), None), P(("ctx", "uly"), None))
    return jax.shard_map(
        on_device, mesh=mesh, in_specs=placed, out_specs=P(("ctx", "uly"), None), check_vma=False
    )
```

time: 232 us -> 164 us (0.71)
  matrix products: 93.9 us -> 0 us
  Pallas kernels: 0 us -> 77 us
  other arithmetic: 22.6 us -> 2.11 us
  local copies, waits for them, and re-layouts: 24.1 us -> 4.17 us
  blocking collectives: 21.8 us -> 41.6 us
  loops' own time: 17.1 us -> 0 us
  starting transfers between devices: 34.9 us -> 18.6 us
  waiting for transfers between devices: 15.8 us -> 18.2 us
    dot_general x64 -> x0, matrix products: 93.9 us -> none  [the longest x32 61.3 us: per_item(): jnp.einsum('qt,td->qd', weights.astype(jnp.bfloat16), value_rows, preferr...]
    pallas_call x0 -> x1, Pallas kernels: none -> 77 us  [attend(): pl.pallas_call(kernel, grid_spec=grid_spec, out_shape=jax.ShapeDtypeStruc...]
    all_to_all x0 -> x2, blocking collectives: none -> 22.3 us  [the longest x1 12.5 us: on_device(): lax.all_to_all(keys, 'uly', split_axis=1, concat_axis=0, tiled=True)]
    reduce_sum x32 -> x0, other arithmetic: 21.1 us -> none  [per_item(): new_sum = running_sum * factor + jnp.sum(weights, axis=-1)]
    another operation x4 -> x0, loops' own time: 17.1 us -> none  [absorb(): lax.map(per_item, (jnp.arange(item_count, dtype=jnp.int32), carry_state[0...]
    all_to_all x2 -> x0, waiting for transfers between devices: 11.1 us -> none  [the longest x1 5.55 us: on_device(): lax.all_to_all(values, 'uly', split_axis=1, concat_axis=0, tiled=True)]
    all_to_all x1, waiting for transfers between devices: 0.01 us -> 9.68 us  [on_device(): lax.all_to_all(queries, 'uly', split_axis=1, concat_axis=0, tiled=True)]
    all_to_all x2 -> x0, starting transfers between devices: 8.72 us -> none  [the longest x1 5.31 us: on_device(): lax.all_to_all(keys, 'uly', split_axis=1, concat_axis=0, tiled=True)]
  transfers between devices with their start and end apart: 9 -> 7, of which waited for: 4 -> 4; matrix products, arithmetic and copies ran while one was open for 45% -> 2% of each run, Pallas kernels for 0% -> 0%
where the time goes in v1:
time: 164 us; the launch traced here: 162 us
  Pallas kernels  77 us (47%)
  blocking collectives  41.6 us (25%)
  starting transfers between devices  18.6 us (11%)
  waiting for transfers between devices  18.2 us (11%)
  local copies, waits for them, and re-layouts  4.17 us (3%)
  other arithmetic  2.11 us (1%)
    pallas_call x1, Pallas kernels, attend(): pl.pallas_call(kernel, grid_spec=grid_spec, out_shape=jax.ShapeDtypeStruc...  77 us
    all_to_all x1, blocking collectives, on_device(): lax.all_to_all(output_rows, 'uly', split_axis=0, concat_axis=1, tiled=True)  19.3 us
    ppermute x6, starting transfers between devices, passed_along(): return lax.ppermute(block, axis, route)  15 us
    all_to_all x1, blocking collectives, on_device(): lax.all_to_all(keys, 'uly', split_axis=1, concat_axis=0, tiled=True)  12.5 us
    all_to_all x1, blocking collectives, on_device(): lax.all_to_all(values, 'uly', split_axis=1, concat_axis=0, tiled=True)  9.89 us
    all_to_all x1, waiting for transfers between devices, on_device(): lax.all_to_all(queries, 'uly', split_axis=1, concat_axis=0, tiled=True)  9.68 us
    ppermute x6, waiting for transfers between devices, passed_along(): return lax.ppermute(block, axis, route)  8.56 us
    all_to_all x1, starting transfers between devices, on_device(): lax.all_to_all(queries, 'uly', split_axis=1, concat_axis=0, tiled=True)  3.56 us
  transfers between devices with their start and end apart: 7, of which 4 were waited for; matrix products, arithmetic and copies ran while one was open for 2% of the time, Pallas kernels for 0%

profile of v1, /device:TPU:224, one launch (start us, length us, event | category | flops | bytes accessed | tf_op | source)
XLA Modules:
  0.0 161.8 jit_solution(11820015590163630521)
XLA Ops:
  0.0 0.0 copy-start
  0.0 0.0 copy-start.3
  0.0 0.9 copy-done
  1.0 0.0 copy-start.2
  1.0 12.5 %all_to_all.76 = bf16[128,8,128]{2,0,1:T(8,128)(2,1)S(1)} all-to-all(bf16[128,8,128]{2,0,1:T(8,128)(2,1)S(1)} %copy_bitcast_fusion.2), channel_id=1, replica_groups=mesh['ctx'=32,'uly'=8] {'uly'}, dimensions={1} | all-to-all | bytes 524288 | tf_op jit(solution)/shard_map/all_to_all | solution.py:99
  13.5 1.9 %collective-permute-start = (bf16[1024,128]{1,0:T(8,128)(2,1)S(1)}, bf16[1024,128]{1,0:T(8,128)(2,1)S(1)}, u32[]{:S(2)}, u32[]{:S(2)}) collective-permute-start(bf16[1024,128]{1,0:T(8,128)(2,1)S(1)} %bitcast.34), channel_id=1, source_target_pairs={{0,8},{8,16},{16,24},{24,32},{32,40},{40,48},{48,56},{56,64},{64,7... | collective-permute-start | bytes 786440 | tf_op jit(solution)/shard_map/ppermute | solution.py:18
  15.4 0.0 copy-done.3
  15.4 9.9 %all_to_all.77 = bf16[128,8,128]{2,0,1:T(8,128)(2,1)S(1)} all-to-all(bf16[128,8,128]{2,0,1:T(8,128)(2,1)S(1)} %copy_bitcast_fusion.1), channel_id=1, replica_groups=mesh['ctx'=32,'uly'=8] {'uly'}, dimensions={1} | all-to-all | bytes 524288 | tf_op jit(solution)/shard_map/all_to_all | solution.py:100
  25.3 1.9 %collective-permute-start.3 = (bf16[1024,128]{1,0:T(8,128)(2,1)S(1)}, bf16[1024,128]{1,0:T(8,128)(2,1)S(1)}, u32[]{:S(2)}, u32[]{:S(2)}) collective-permute-start(bf16[1024,128]{1,0:T(8,128)(2,1)S(1)} %bitcast.32), channel_id=1, source_target_pairs={{0,8},{8,16},{16,24},{24,32},{32,40},{40,48},{48,56},{56,64},{64,7... | collective-permute-start | bytes 786440 | tf_op jit(solution)/shard_map/ppermute | solution.py:18
  27.2 0.0 collective-permute-done
  27.3 1.9 %collective-permute-start.1 = (bf16[1024,128]{1,0:T(8,128)(2,1)S(1)}, bf16[1024,128]{1,0:T(8,128)(2,1)S(1)}, u32[]{:S(2)}, u32[]{:S(2)}) collective-permute-start(bf16[1024,128]{1,0:T(8,128)(2,1)S(1)} %collective-permute-done), channel_id=1, source_target_pairs={{0,8},{8,16},{16,24},{24,32},{32,40},{40,48},{48,56},{56,64},{64,7... | collective-permute-start | bytes 786440 | tf_op jit(solution)/shard_map/ppermute | solution.py:18
  29.2 3.8 %collective-permute-done.3 = bf16[1024,128]{1,0:T(8,128)(2,1)S(1)} collective-permute-done((bf16[1024,128]{1,0:T(8,128)(2,1)S(1)}, bf16[1024,128]{1,0:T(8,128)(2,1)S(1)}, u32[]{:S(2)}, u32[]{:S(2)}) %collective-permute-start.3) | collective-permute-done | bytes 262176 | tf_op jit(solution)/shard_map/ppermute | solution.py:18
  33.0 1.9 %collective-permute-start.4 = (bf16[1024,128]{1,0:T(8,128)(2,1)S(1)}, bf16[1024,128]{1,0:T(8,128)(2,1)S(1)}, u32[]{:S(2)}, u32[]{:S(2)}) collective-permute-start(bf16[1024,128]{1,0:T(8,128)(2,1)S(1)} %collective-permute-done.3), channel_id=1, source_target_pairs={{0,8},{8,16},{16,24},{24,32},{32,40},{40,48},{48,56},{56,64},{64,7... | collective-permute-start | bytes 786440 | tf_op jit(solution)/shard_map/ppermute | solution.py:18
  34.9 0.9 collective-permute-done.1
  35.8 4.6 %collective-permute-start.2 = (bf16[1024,128]{1,0:T(8,128)(2,1)S(1)}, bf16[1024,128]{1,0:T(8,128)(2,1)S(1)}, u32[]{:S(2)}, u32[]{:S(2)}) collective-permute-start(bf16[1024,128]{1,0:T(8,128)(2,1)S(1)} %collective-permute-done.1), channel_id=1, source_target_pairs={{0,8},{8,16},{16,24},{24,32},{32,40},{40,48},{48,56},{56,64},{64,7... | collective-permute-start | bytes 786440 | tf_op jit(solution)/shard_map/ppermute | solution.py:18
  40.4 0.0 copy-done.2
  40.4 1.1 copy.15
  41.5 3.6 %all-to-all-start = ((bf16[128,8,512]{2,0,1:T(8,128)(2,1)}), bf16[128,8,512]{2,0,1:T(8,128)(2,1)S(1)}, u32[]{:S(2)}, u32[]{:S(2)}) async-start(bf16[128,8,512]{2,0,1:T(8,128)(2,1)} %bitcast.27), calls=%async_computation | async-start | bytes 2097152 | tf_op jit(solution)/shard_map/all_to_all | solution.py:98
  45.0 0.0 collective-permute-done.4
  45.1 2.8 %collective-permute-start.5 = (bf16[1024,128]{1,0:T(8,128)(2,1)S(1)}, bf16[1024,128]{1,0:T(8,128)(2,1)S(1)}, u32[]{:S(2)}, u32[]{:S(2)}) collective-permute-start(bf16[1024,128]{1,0:T(8,128)(2,1)S(1)} %collective-permute-done.4), channel_id=1, source_target_pairs={{0,8},{8,16},{16,24},{24,32},{32,40},{40,48},{48,56},{56,64},{64,7... | collective-permute-start | bytes 786440 | tf_op jit(solution)/shard_map/ppermute | solution.py:18
  47.9 0.0 collective-permute-done.2
  47.9 1.0 pad_maximum_fusion.k_ref
  48.9 3.8 %collective-permute-done.5 = bf16[1024,128]{1,0:T(8,128)(2,1)S(1)} collective-permute-done((bf16[1024,128]{1,0:T(8,128)(2,1)S(1)}, bf16[1024,128]{1,0:T(8,128)(2,1)S(1)}, u32[]{:S(2)}, u32[]{:S(2)}) %collective-permute-start.5) | collective-permute-done | bytes 262176 | tf_op jit(solution)/shard_map/ppermute | solution.py:18
  52.8 1.1 pad_maximum_fusion.1.v_ref
  53.8 9.7 %all-to-all-done = bf16[128,8,512]{2,0,1:T(8,128)(2,1)S(1)} async-done(((bf16[128,8,512]{2,0,1:T(8,128)(2,1)}), bf16[128,8,512]{2,0,1:T(8,128)(2,1)S(1)}, u32[]{:S(2)}, u32[]{:S(2)}) %all-to-all-start) | async-done | bytes 1048608 | tf_op jit(solution)/shard_map/all_to_all | solution.py:98
  63.5 0.0 copy-start.1
  63.5 1.0 copy-done.1
  64.5 77.0 %shard_map.37 = bf16[1024,512]{1,0:T(8,128)(2,1)} custom-call(s32[1]{0:T(128)} %bitcast.pos_ref, bf16[1024,512]{1,0:T(8,128)(2,1)} %bitcast.28, bf16[4096,128]{1,0:T(8,128)(2,1)} %pad_maximum_fusion.k_ref, bf16[4096,128]{1,0:T(8,128)(2,1)} %pad_maximum_fusion.1.v_ref), custom_call_target="tpu_custom_call" | custom-call | tf_op jit(solution)/shard_map/pallas_call | solution.py:87
  141.5 19.3 %all_to_all.78 = bf16[8,128,512]{2,1,0:T(8,128)(2,1)S(1)} all-to-all(bf16[8,128,512]{2,1,0:T(8,128)(2,1)} %bitcast.29), channel_id=1, replica_groups=mesh['ctx'=32,'uly'=8] {'uly'}, dimensions={0} | all-to-all | bytes 2097152 | tf_op jit(solution)/shard_map/all_to_all | solution.py:113
  160.8 1.1 copy.11
  (2 shorter events, 0.1 us)
Async XLA Ops:
  0.0 1.0 copy-start
  0.0 15.4 %copy-start.3 = (bf16[128,1024]{1,0:T(8,128)(2,1)S(1)}, bf16[128,1024]{1,0:T(8,128)(2,1)}, u32[]{:S(2)}) copy-start(bf16[128,1024]{1,0:T(8,128)(2,1)} %param.5) | copy-start | bytes 786436
  1.0 39.4 %copy-start.2 = (bf16[128,4096]{1,0:T(8,128)(2,1)S(1)}, bf16[128,4096]{1,0:T(8,128)(2,1)}, u32[]{:S(2)}) copy-start(bf16[128,4096]{1,0:T(8,128)(2,1)} %param.3) | copy-start | bytes 3145732
  13.5 13.8 %collective-permute-start = (bf16[1024,128]{1,0:T(8,128)(2,1)S(1)}, bf16[1024,128]{1,0:T(8,128)(2,1)S(1)}, u32[]{:S(2)}, u32[]{:S(2)}) collective-permute-start(bf16[1024,128]{1,0:T(8,128)(2,1)S(1)} %bitcast.34), channel_id=1, source_target_pairs={{0,8},{8,16},{16,24},{24,32},{32,40},{40,48},{48,56},{56,64},{64,7... | collective-permute-start | bytes 786440 | tf_op jit(solution)/shard_map/ppermute | solution.py:18
  25.3 7.7 %collective-permute-start.3 = (bf16[1024,128]{1,0:T(8,128)(2,1)S(1)}, bf16[1024,128]{1,0:T(8,128)(2,1)S(1)}, u32[]{:S(2)}, u32[]{:S(2)}) collective-permute-start(bf16[1024,128]{1,0:T(8,128)(2,1)S(1)} %bitcast.32), channel_id=1, source_target_pairs={{0,8},{8,16},{16,24},{24,32},{32,40},{40,48},{48,56},{56,64},{64,7... | collective-permute-start | bytes 786440 | tf_op jit(solution)/shard_map/ppermute | solution.py:18
  27.3 8.6 %collective-permute-start.1 = (bf16[1024,128]{1,0:T(8,128)(2,1)S(1)}, bf16[1024,128]{1,0:T(8,128)(2,1)S(1)}, u32[]{:S(2)}, u32[]{:S(2)}) collective-permute-start(bf16[1024,128]{1,0:T(8,128)(2,1)S(1)} %collective-permute-done), channel_id=1, source_target_pairs={{0,8},{8,16},{16,24},{24,32},{32,40},{40,48},{48,56},{56,64},{64,7... | collective-permute-start | bytes 786440 | tf_op jit(solution)/shard_map/ppermute | solution.py:18
  33.0 12.0 %collective-permute-start.4 = (bf16[1024,128]{1,0:T(8,128)(2,1)S(1)}, bf16[1024,128]{1,0:T(8,128)(2,1)S(1)}, u32[]{:S(2)}, u32[]{:S(2)}) collective-permute-start(bf16[1024,128]{1,0:T(8,128)(2,1)S(1)} %collective-permute-done.3), channel_id=1, source_target_pairs={{0,8},{8,16},{16,24},{24,32},{32,40},{40,48},{48,56},{56,64},{64,7... | collective-permute-start | bytes 786440 | tf_op jit(solution)/shard_map/ppermute | solution.py:18
  35.8 12.0 %collective-permute-start.2 = (bf16[1024,128]{1,0:T(8,128)(2,1)S(1)}, bf16[1024,128]{1,0:T(8,128)(2,1)S(1)}, u32[]{:S(2)}, u32[]{:S(2)}) collective-permute-start(bf16[1024,128]{1,0:T(8,128)(2,1)S(1)} %collective-permute-done.1), channel_id=1, source_target_pairs={{0,8},{8,16},{16,24},{24,32},{32,40},{40,48},{48,56},{56,64},{64,7... | collective-permute-start | bytes 786440 | tf_op jit(solution)/shard_map/ppermute | solution.py:18
  41.5 22.0 %all-to-all-start = ((bf16[128,8,512]{2,0,1:T(8,128)(2,1)}), bf16[128,8,512]{2,0,1:T(8,128)(2,1)S(1)}, u32[]{:S(2)}, u32[]{:S(2)}) async-start(bf16[128,8,512]{2,0,1:T(8,128)(2,1)} %bitcast.27), calls=%async_computation | async-start | bytes 2097152 | tf_op jit(solution)/shard_map/all_to_all | solution.py:98
  45.1 7.7 %collective-permute-start.5 = (bf16[1024,128]{1,0:T(8,128)(2,1)S(1)}, bf16[1024,128]{1,0:T(8,128)(2,1)S(1)}, u32[]{:S(2)}, u32[]{:S(2)}) collective-permute-start(bf16[1024,128]{1,0:T(8,128)(2,1)S(1)} %collective-permute-done.4), channel_id=1, source_target_pairs={{0,8},{8,16},{16,24},{24,32},{32,40},{40,48},{48,56},{56,64},{64,7... | collective-permute-start | bytes 786440 | tf_op jit(solution)/shard_map/ppermute | solution.py:18
  63.5 1.0 copy-start.1

commit v2 on v1

v2 whole, which is shorter than its diff:
```python
import functools

import jax
import jax.numpy as jnp
from jax import lax
from jax.experimental import pallas as pl
from jax.experimental.pallas import tpu as pltpu
from jax.sharding import PartitionSpec as P

HEAD_SIZE = 128
WINDOW_BLOCKS = 3
KEY_TILE = 1024
LOG2_E = 1.4426950408889634


def passed_along(block, axis, distance):
    devices = range(lax.axis_size(axis))
    route = [(i - distance, i) for i in devices if i - distance in devices]
    return lax.ppermute(block, axis, route)


def attend_kernel(pos_ref, q_ref, kv0_ref, kv1_ref, kv2_ref, kv3_ref, o_ref, m_ref, l_ref, acc_ref, *, block_len):
    cycle_pos = pos_ref[0]
    exp_scale = HEAD_SIZE ** (-0.5) * LOG2_E
    q = q_ref[...]
    tile = min(KEY_TILE, block_len)
    m_ref[...] = jnp.full(m_ref.shape, -jnp.inf, jnp.float32)
    l_ref[...] = jnp.zeros(l_ref.shape, jnp.float32)
    acc_ref[...] = jnp.zeros(acc_ref.shape, jnp.float32)

    def process(kv_ref, start, masked):
        k = kv_ref[pl.ds(start, tile), pl.ds(0, HEAD_SIZE)]
        v = kv_ref[pl.ds(start, tile), pl.ds(HEAD_SIZE, HEAD_SIZE)]
        s = lax.dot_general(k, q, (((1,), (1,)), ((), ())), preferred_element_type=jnp.float32)
        if masked:
            keys = lax.broadcasted_iota(jnp.int32, s.shape, 0) + start
            rows = lax.broadcasted_iota(jnp.int32, s.shape, 1)
            s = jnp.where(keys <= rows, s, jnp.float32(-1e30))
        m_old = m_ref[...]
        m_new = jnp.maximum(m_old, jnp.max(s, axis=0, keepdims=True))
        p = jnp.exp2((s - m_new) * exp_scale)
        factor = jnp.exp2((m_old - m_new) * exp_scale)
        l_ref[...] = l_ref[...] * factor + jnp.sum(p, axis=0, keepdims=True)
        pv = lax.dot_general(
            v, p.astype(jnp.bfloat16), (((0,), (0,)), ((), ())), preferred_element_type=jnp.float32
        )
        acc_ref[...] = acc_ref[...] * factor + pv
        m_ref[...] = m_new

    for t in range(block_len // tile):
        process(kv3_ref, t * tile, True)
    for back, kv_ref in ((1, kv2_ref), (2, kv1_ref), (3, kv0_ref)):
        @pl.when(cycle_pos >= back)
        def _():
            for t in range(block_len // tile):
                process(kv_ref, t * tile, False)

    o_ref[...] = (acc_ref[...] / l_ref[...]).T.astype(o_ref.dtype)


def attend(pos, qkv, kv0, kv1, kv2, q_heads):
    block_len = qkv.shape[0]
    kernel = functools.partial(attend_kernel, block_len=block_len)
    kv_spec = pl.BlockSpec((block_len, 2 * HEAD_SIZE), lambda h, pos: (0, 0))
    grid_spec = pltpu.PrefetchScalarGridSpec(
        num_scalar_prefetch=1,
        grid=(q_heads,),
        in_specs=[
            pl.BlockSpec((block_len, HEAD_SIZE), lambda h, pos: (0, h)),
            kv_spec,
            kv_spec,
            kv_spec,
            pl.BlockSpec((block_len, 2 * HEAD_SIZE), lambda h, pos: (0, q_heads // 2)),
        ],
        out_specs=pl.BlockSpec((block_len, HEAD_SIZE), lambda h, pos: (0, h)),
        scratch_shapes=[
            pltpu.VMEM((1, block_len), jnp.float32),
            pltpu.VMEM((1, block_len), jnp.float32),
            pltpu.VMEM((HEAD_SIZE, block_len), jnp.float32),
        ],
    )
    return pl.pallas_call(
        kernel,
        grid_spec=grid_spec,
        out_shape=jax.ShapeDtypeStruct((block_len, q_heads * HEAD_SIZE), jnp.bfloat16),
        compiler_params=pltpu.CompilerParams(dimension_semantics=("arbitrary",)),
    )(pos, qkv, kv0, kv1, kv2, qkv)


def on_device(queries, keys, values):
    n = lax.axis_size("uly")
    rows = queries.shape[0]
    cycle_pos = lax.axis_index("ctx")
    packed = jnp.concatenate(
        [queries.reshape(rows, n, -1), keys.reshape(rows, n, -1), values.reshape(rows, n, -1)], axis=2
    )
    qkv = lax.all_to_all(packed, "uly", split_axis=1, concat_axis=0, tiled=True)
    qkv = qkv.reshape(rows * n, -1)
    q_heads = (qkv.shape[1] - 2 * HEAD_SIZE) // HEAD_SIZE
    kv_own = qkv[:, q_heads * HEAD_SIZE:]
    kv1 = passed_along(kv_own, "ctx", 1)
    kv2 = passed_along(kv1, "ctx", 1)
    kv3 = passed_along(kv2, "ctx", 1)
    pos = jnp.reshape(cycle_pos, (1,)).astype(jnp.int32)
    output_rows = attend(pos, qkv, kv3, kv2, kv1, q_heads)
    return lax.all_to_all(output_rows, "uly", split_axis=0, concat_axis=1, tiled=True)


def solution(mesh):
    placed = (P(("ctx", "uly"), None), P(("ctx", "uly"), None), P(("ctx", "uly"), None))
    return jax.shard_map(
        on_device, mesh=mesh, in_specs=placed, out_specs=P(("ctx", "uly"), None), check_vma=False
    )
```

time: 164 us -> 119 us (0.73)
  the two profiles are of different devices: /device:TPU:224 before, /device:TPU:16 now
where the time goes in v2:
time: 119 us
  blocking collectives  40.4 us (34%)
  waiting for transfers between devices  37.3 us (31%)
  Pallas kernels  31.7 us (27%)
  starting transfers between devices  5.74 us (5%)
  local copies, waits for them, and re-layouts  3.39 us (3%)
    ppermute x3, waiting for transfers between devices, passed_along(): return lax.ppermute(block, axis, route)  37.3 us
    pallas_call x1, Pallas kernels, attend(): pl.pallas_call(kernel, grid_spec=grid_spec, out_shape=jax.ShapeDtypeStruc...  31.7 us
    all_to_all x1, blocking collectives, on_device(): qkv = lax.all_to_all(packed, 'uly', split_axis=1, concat_axis=0, tiled=True)  25.8 us
    all_to_all x1, blocking collectives, on_device(): lax.all_to_all(output_rows, 'uly', split_axis=0, concat_axis=1, tiled=True)  14.6 us
    ppermute x3, starting transfers between devices, passed_along(): return lax.ppermute(block, axis, route)  5.74 us
  transfers between devices with their start and end apart: 3, of which 3 were waited for; matrix products, arithmetic and copies ran while one was open for 0% of the time, Pallas kernels for 0%

profile of v2, /device:TPU:16, one launch (start us, length us, event | category | flops | bytes accessed | tf_op | source)
XLA Modules:
  0.0 118.7 jit_solution(9047116793387741372)
XLA Ops:
  0.0 0.0 copy-start
  0.0 0.0 copy-start.5
  0.0 1.4 %copy.15 = bf16[16,8,8,512]{3,2,0,1:T(8,128)(2,1)S(1)} copy(bf16[16,8,8,512]{3,2,1,0:T(8,128)(2,1)} %bitcast.30) | data formatting | bytes 2097152 | tf_op jit(solution)/shard_map/reshape | solution.py:95
  1.4 0.0 copy-done
  1.4 0.0 copy-done.5
  1.4 0.1 copy_bitcast_fusion.1
  1.5 0.1 pad_maximum_fusion
  1.7 25.8 %all_to_all.34 = bf16[128,8,768]{2,0,1:T(8,128)(2,1)S(1)} all-to-all(bf16[128,8,768]{2,0,1:T(8,128)(2,1)S(1)} %pad_maximum_fusion), channel_id=1, replica_groups=mesh['ctx'=32,'uly'=8] {'uly'}, dimensions={1} | all-to-all | bytes 3145728 | tf_op jit(solution)/shard_map/all_to_all | solution.py:97
  27.5 0.0 copy-start.1
  27.5 1.9 %collective-permute-start = (bf16[1024,256]{1,0:T(8,128)(2,1)S(1)}, bf16[1024,256]{1,0:T(8,128)(2,1)S(1)}, u32[]{:S(2)}, u32[]{:S(2)}) collective-permute-start(bf16[1024,256]{1,0:T(8,128)(2,1)S(1)} %slice.4), channel_id=1, source_target_pairs={{0,8},{8,16},{16,24},{24,32},{32,40},{40,48},{48,56},{56,64},{64,7... | collective-permute-start | bytes 1572872 | tf_op jit(solution)/shard_map/ppermute | solution.py:19
  29.4 12.2 %collective-permute-done.kv2_ref = bf16[1024,256]{1,0:T(8,128)(2,1)S(1)} collective-permute-done((bf16[1024,256]{1,0:T(8,128)(2,1)S(1)}, bf16[1024,256]{1,0:T(8,128)(2,1)S(1)}, u32[]{:S(2)}, u32[]{:S(2)}) %collective-permute-start) | collective-permute-done | bytes 524320 | tf_op jit(solution)/shard_map/ppermute | solution.py:19
  41.6 0.0 copy-start.2
  41.6 1.9 %collective-permute-start.1 = (bf16[1024,256]{1,0:T(8,128)(2,1)S(1)}, bf16[1024,256]{1,0:T(8,128)(2,1)S(1)}, u32[]{:S(2)}, u32[]{:S(2)}) collective-permute-start(bf16[1024,256]{1,0:T(8,128)(2,1)S(1)} %collective-permute-done.kv2_ref), channel_id=1, source_target_pairs={{0,8},{8,16},{16,24},{24,32},{32,40},{40,48},{48,56},{56,64},{64,7... | collective-permute-start | bytes 1572872 | tf_op jit(solution)/shard_map/ppermute | solution.py:19
  43.5 12.2 %collective-permute-done.1.kv1_ref = bf16[1024,256]{1,0:T(8,128)(2,1)S(1)} collective-permute-done((bf16[1024,256]{1,0:T(8,128)(2,1)S(1)}, bf16[1024,256]{1,0:T(8,128)(2,1)S(1)}, u32[]{:S(2)}, u32[]{:S(2)}) %collective-permute-start.1) | collective-permute-done | bytes 524320 | tf_op jit(solution)/shard_map/ppermute | solution.py:19
  55.7 0.0 copy-start.3
  55.7 1.9 %collective-permute-start.2 = (bf16[1024,256]{1,0:T(8,128)(2,1)S(1)}, bf16[1024,256]{1,0:T(8,128)(2,1)S(1)}, u32[]{:S(2)}, u32[]{:S(2)}) collective-permute-start(bf16[1024,256]{1,0:T(8,128)(2,1)S(1)} %collective-permute-done.1.kv1_ref), channel_id=1, source_target_pairs={{0,8},{8,16},{16,24},{24,32},{32,40},{40,48},{48,56},{56,64},{64,7... | collective-permute-start | bytes 1572872 | tf_op jit(solution)/shard_map/ppermute | solution.py:19
  57.6 12.9 %collective-permute-done.2.kv0_ref = bf16[1024,256]{1,0:T(8,128)(2,1)S(1)} collective-permute-done((bf16[1024,256]{1,0:T(8,128)(2,1)S(1)}, bf16[1024,256]{1,0:T(8,128)(2,1)S(1)}, u32[]{:S(2)}, u32[]{:S(2)}) %collective-permute-start.2) | collective-permute-done | bytes 524320 | tf_op jit(solution)/shard_map/ppermute | solution.py:19
  70.5 0.0 copy-start.4
  70.5 0.0 copy-done.1
  70.5 0.0 copy-done.2
  70.5 0.0 copy-done.3
  70.5 0.8 copy-done.4
  71.3 31.7 %shard_map.37 = bf16[1024,512]{1,0:T(8,128)(2,1)} custom-call(s32[1]{0:T(128)} %bitcast.pos_ref, bf16[1024,768]{1,0:T(8,128)(2,1)} %bitcast.25, bf16[1024,256]{1,0:T(8,128)(2,1)} %copy-done.4, bf16[1024,256]{1,0:T(8,128)(2,1)} %copy-done.3, bf16[1024,256]{1,0:T(8,128)(2,1)} %copy-done.2, bf16[1024,768]{1,0:T(8,128)(2,1)} %bitcast.26), custom_call_target="tpu_custom_call" | custom-call | tf_op jit(solution)/shard_map/pallas_call | solution.py:82
  103.0 14.6 %all_to_all.35 = bf16[8,128,512]{2,1,0:T(8,128)(2,1)S(1)} all-to-all(bf16[8,128,512]{2,1,0:T(8,128)(2,1)} %bitcast.29), channel_id=1, replica_groups=mesh['ctx'=32,'uly'=8] {'uly'}, dimensions={0} | all-to-all | bytes 2097152 | tf_op jit(solution)/shard_map/all_to_all | solution.py:106
  117.6 1.1 copy.11
  (1 shorter events, 0.0 us)
Async XLA Ops:
  0.0 1.4 %copy-start = (bf16[128,1024]{1,0:T(8,128)(2,1)S(1)}, bf16[128,1024]{1,0:T(8,128)(2,1)}, u32[]{:S(2)}) copy-start(bf16[128,1024]{1,0:T(8,128)(2,1)} %param.4) | copy-start | bytes 786436
  0.0 1.4 %copy-start.5 = (bf16[128,1024]{1,0:T(8,128)(2,1)S(1)}, bf16[128,1024]{1,0:T(8,128)(2,1)}, u32[]{:S(2)}) copy-start(bf16[128,1024]{1,0:T(8,128)(2,1)} %param.5) | copy-start | bytes 786436
  27.5 43.1 %copy-start.1 = (bf16[128,8,768]{2,0,1:T(8,128)(2,1)}, bf16[128,8,768]{2,0,1:T(8,128)(2,1)S(1)}, u32[]{:S(2)}) copy-start(bf16[128,8,768]{2,0,1:T(8,128)(2,1)S(1)} %all_to_all.34) | copy-start | bytes 4718596
  27.5 14.1 %collective-permute-start = (bf16[1024,256]{1,0:T(8,128)(2,1)S(1)}, bf16[1024,256]{1,0:T(8,128)(2,1)S(1)}, u32[]{:S(2)}, u32[]{:S(2)}) collective-permute-start(bf16[1024,256]{1,0:T(8,128)(2,1)S(1)} %slice.4), channel_id=1, source_target_pairs={{0,8},{8,16},{16,24},{24,32},{32,40},{40,48},{48,56},{56,64},{64,7... | collective-permute-start | bytes 1572872 | tf_op jit(solution)/shard_map/ppermute | solution.py:19
  41.6 28.9 %copy-start.2 = (bf16[1024,256]{1,0:T(8,128)(2,1)}, bf16[1024,256]{1,0:T(8,128)(2,1)S(1)}, u32[]{:S(2)}) copy-start(bf16[1024,256]{1,0:T(8,128)(2,1)S(1)} %collective-permute-done.kv2_ref) | copy-start | bytes 1572868
  41.6 14.1 %collective-permute-start.1 = (bf16[1024,256]{1,0:T(8,128)(2,1)S(1)}, bf16[1024,256]{1,0:T(8,128)(2,1)S(1)}, u32[]{:S(2)}, u32[]{:S(2)}) collective-permute-start(bf16[1024,256]{1,0:T(8,128)(2,1)S(1)} %collective-permute-done.kv2_ref), channel_id=1, source_target_pairs={{0,8},{8,16},{16,24},{24,32},{32,40},{40,48},{48,56},{56,64},{64,7... | collective-permute-start | bytes 1572872 | tf_op jit(solution)/shard_map/ppermute | solution.py:19
  55.7 14.8 %copy-start.3 = (bf16[1024,256]{1,0:T(8,128)(2,1)}, bf16[1024,256]{1,0:T(8,128)(2,1)S(1)}, u32[]{:S(2)}) copy-start(bf16[1024,256]{1,0:T(8,128)(2,1)S(1)} %collective-permute-done.1.kv1_ref) | copy-start | bytes 1572868
  55.7 14.8 %collective-permute-start.2 = (bf16[1024,256]{1,0:T(8,128)(2,1)S(1)}, bf16[1024,256]{1,0:T(8,128)(2,1)S(1)}, u32[]{:S(2)}, u32[]{:S(2)}) collective-permute-start(bf16[1024,256]{1,0:T(8,128)(2,1)S(1)} %collective-permute-done.1.kv1_ref), channel_id=1, source_target_pairs={{0,8},{8,16},{16,24},{24,32},{32,40},{40,48},{48,56},{56,64},{64,7... | collective-permute-start | bytes 1572872 | tf_op jit(solution)/shard_map/ppermute | solution.py:19
  70.5 0.8 copy-start.4

commit v3 on v2

v3 whole, which is shorter than its diff:
```python
import functools

import jax
import jax.numpy as jnp
from jax import lax
from jax.experimental import pallas as pl
from jax.experimental.pallas import tpu as pltpu
from jax.sharding import PartitionSpec as P


HEAD_SIZE = 128
WINDOW_BLOCKS = 3
KEY_TILE = 1024
LOG2_E = 1.4426950408889634


def passed_along(block, axis, distance):
    devices = range(lax.axis_size(axis))
    route = [(i - distance, i) for i in devices if i - distance in devices]
    return lax.ppermute(block, axis, route)


def attend_kernel(pos_ref, q_ref, kv_ref, *refs, block_len, back, first, last):
    if first:
        o_refs, (m_ref, l_ref, acc_ref) = refs[:-3], refs[-3:]
    else:
        (m_in, l_in, acc_in), o_refs, (m_ref, l_ref, acc_ref) = refs[:3], refs[3:-3], refs[-3:]
    cycle_pos = pos_ref[0]
    exp_scale = HEAD_SIZE ** (-0.5) * LOG2_E
    tile = min(KEY_TILE, block_len)
    if first:
        m_ref[...] = jnp.full(m_ref.shape, -jnp.inf, jnp.float32)
        l_ref[...] = jnp.zeros(l_ref.shape, jnp.float32)
        acc_ref[...] = jnp.zeros(acc_ref.shape, jnp.float32)
    else:
        m_ref[...] = m_in[...]
        l_ref[...] = l_in[...]
        acc_ref[...] = acc_in[...]

    def process(start, masked):
        q = q_ref[...]
        k = kv_ref[pl.ds(start, tile), pl.ds(0, HEAD_SIZE)]
        v = kv_ref[pl.ds(start, tile), pl.ds(HEAD_SIZE, HEAD_SIZE)]
        s = lax.dot_general(k, q, (((1,), (1,)), ((), ())), preferred_element_type=jnp.float32)
        if masked:
            keys = lax.broadcasted_iota(jnp.int32, s.shape, 0) + start
            rows = lax.broadcasted_iota(jnp.int32, s.shape, 1)
            s = jnp.where(keys <= rows, s, jnp.float32(-1e30))
        m_old = m_ref[...]
        m_new = jnp.maximum(m_old, jnp.max(s, axis=0, keepdims=True))
        p = jnp.exp2((s - m_new) * exp_scale)
        factor = jnp.exp2((m_old - m_new) * exp_scale)
        l_ref[...] = l_ref[...] * factor + jnp.sum(p, axis=0, keepdims=True)
        pv = lax.dot_general(
            v, p.astype(jnp.bfloat16), (((0,), (0,)), ((), ())), preferred_element_type=jnp.float32
        )
        acc_ref[...] = acc_ref[...] * factor + pv
        m_ref[...] = m_new

    if back == 0:
        for t in range(block_len // tile):
            process(t * tile, True)
    else:
        @pl.when(cycle_pos >= back)
        def _():
            for t in range(block_len // tile):
                process(t * tile, False)

    if last:
        o_refs[0][...] = (acc_ref[...] / l_ref[...]).T.astype(o_refs[0].dtype)
    else:
        o_refs[0][...] = m_ref[...]
        o_refs[1][...] = l_ref[...]
        o_refs[2][...] = acc_ref[...]


def attend(pos, qkv, kv, carry, q_heads, back, kv_col):
    block_len = qkv.shape[0]
    first = carry is None
    last = back == WINDOW_BLOCKS
    kernel = functools.partial(attend_kernel, block_len=block_len, back=back, first=first, last=last)
    row_spec = pl.BlockSpec((None, 1, block_len), lambda h, pos: (h, 0, 0))
    acc_spec = pl.BlockSpec((None, HEAD_SIZE, block_len), lambda h, pos: (h, 0, 0))
    in_specs = [
        pl.BlockSpec((block_len, HEAD_SIZE), lambda h, pos: (0, h)),
        pl.BlockSpec((block_len, 2 * HEAD_SIZE), lambda h, pos: (0, kv_col)),
    ]
    operands = [pos, qkv, kv]
    if not first:
        in_specs += [row_spec, row_spec, acc_spec]
        operands += list(carry)
    carry_shapes = [
        jax.ShapeDtypeStruct((q_heads, 1, block_len), jnp.float32),
        jax.ShapeDtypeStruct((q_heads, 1, block_len), jnp.float32),
        jax.ShapeDtypeStruct((q_heads, HEAD_SIZE, block_len), jnp.float32),
    ]
    if last:
        out_specs = [pl.BlockSpec((block_len, HEAD_SIZE), lambda h, pos: (0, h))]
        out_shape = [jax.ShapeDtypeStruct((block_len, q_heads * HEAD_SIZE), jnp.bfloat16)]
        aliases = {}
    else:
        out_specs = [row_spec, row_spec, acc_spec]
        out_shape = carry_shapes
        aliases = {} if first else {3: 0, 4: 1, 5: 2}
    grid_spec = pltpu.PrefetchScalarGridSpec(
        num_scalar_prefetch=1,
        grid=(q_heads,),
        in_specs=in_specs,
        out_specs=out_specs,
        scratch_shapes=[
            pltpu.VMEM((1, block_len), jnp.float32),
            pltpu.VMEM((1, block_len), jnp.float32),
            pltpu.VMEM((HEAD_SIZE, block_len), jnp.float32),
        ],
    )
    result = pl.pallas_call(
        kernel,
        grid_spec=grid_spec,
        out_shape=out_shape,
        input_output_aliases=aliases,
        compiler_params=pltpu.CompilerParams(dimension_semantics=("arbitrary",)),
    )(*operands)
    return result[0] if last else tuple(result)


def on_device(queries, keys, values):
    n = lax.axis_size("uly")
    rows = queries.shape[0]
    cycle_pos = lax.axis_index("ctx")
    packed = jnp.concatenate(
        [queries.reshape(rows, n, -1), keys.reshape(rows, n, -1), values.reshape(rows, n, -1)], axis=2
    )
    qkv = lax.all_to_all(packed, "uly", split_axis=1, concat_axis=0, tiled=True)
    qkv = qkv.reshape(rows * n, -1)
    q_heads = (qkv.shape[1] - 2 * HEAD_SIZE) // HEAD_SIZE
    pos = jnp.reshape(cycle_pos, (1,)).astype(jnp.int32)
    kv = qkv[:, q_heads * HEAD_SIZE:]
    carry = attend(pos, qkv, qkv, None, q_heads, 0, q_heads // 2)
    for back in range(1, WINDOW_BLOCKS + 1):
        kv = passed_along(kv, "ctx", 1)
        carry = attend(pos, qkv, kv, carry, q_heads, back, 0)
    return lax.all_to_all(carry, "uly", split_axis=0, concat_axis=1, tiled=True)


def solution(mesh):
    placed = (P(("ctx", "uly"), None), P(("ctx", "uly"), None), P(("ctx", "uly"), None))
    return jax.shard_map(
        on_device, mesh=mesh, in_specs=placed, out_specs=P(("ctx", "uly"), None), check_vma=False
    )
```

time: 119 us -> 114 us (0.958)
  the two profiles are of different devices: /device:TPU:16 before, /device:TPU:97 now
where the time goes in v3:
time: 114 us; the launch traced here: 113 us
  blocking collectives  41.2 us (36%)
  Pallas kernels  38.7 us (34%)
  starting transfers between devices  17.7 us (16%)
  waiting for transfers between devices  12.2 us (11%)
  local copies, waits for them, and re-layouts  3.4 us (3%)
    pallas_call x4, Pallas kernels, attend(): pl.pallas_call(kernel, grid_spec=grid_spec, out_shape=out_shape, input_ou...  38.7 us
    all_to_all x1, blocking collectives, on_device(): qkv = lax.all_to_all(packed, 'uly', split_axis=1, concat_axis=0, tiled=True)  24.9 us
    ppermute x3, starting transfers between devices, passed_along(): return lax.ppermute(block, axis, route)  17.7 us
    all_to_all x1, blocking collectives, on_device(): return lax.all_to_all(carry, 'uly', split_axis=0, concat_axis=1, tiled=True)  16.3 us
    ppermute x3, waiting for transfers between devices, passed_along(): return lax.ppermute(block, axis, route)  12.2 us
  transfers between devices with their start and end apart: 3, of which 2 were waited for; matrix products, arithmetic and copies ran while one was open for 0% of the time, Pallas kernels for 25%

profile of v3, /device:TPU:97, one launch (start us, length us, event | category | flops | bytes accessed | tf_op | source)
XLA Modules:
  0.0 113.5 jit_solution(12508493618772319787)
XLA Ops:
  0.0 0.0 copy-start
  0.0 0.0 copy-start.5
  0.0 1.4 %copy.21 = bf16[16,8,8,512]{3,2,0,1:T(8,128)(2,1)S(1)} copy(bf16[16,8,8,512]{3,2,1,0:T(8,128)(2,1)} %bitcast.33) | data formatting | bytes 2097152 | tf_op jit(solution)/shard_map/reshape | solution.py:131
  1.4 0.0 copy-done
  1.4 0.0 copy-done.5
  1.4 0.1 copy_bitcast_fusion.1
  1.5 0.1 pad_maximum_fusion
  1.7 24.9 %all_to_all.34 = bf16[128,8,768]{2,0,1:T(8,128)(2,1)S(1)} all-to-all(bf16[128,8,768]{2,0,1:T(8,128)(2,1)S(1)} %pad_maximum_fusion), channel_id=1, replica_groups=mesh['ctx'=32,'uly'=8] {'uly'}, dimensions={1} | all-to-all | bytes 3145728 | tf_op jit(solution)/shard_map/all_to_all | solution.py:133
  26.6 0.0 copy-start.1
  26.6 6.5 %collective-permute-start = (bf16[1024,256]{1,0:T(8,128)(2,1)S(1)}, bf16[1024,256]{1,0:T(8,128)(2,1)S(1)}, u32[]{:S(2)}, u32[]{:S(2)}) collective-permute-start(bf16[1024,256]{1,0:T(8,128)(2,1)S(1)} %slice.4), channel_id=1, source_target_pairs={{0,8},{8,16},{16,24},{24,32},{32,40},{40,48},{48,56},{56,64},{64,7... | collective-permute-start | bytes 1572872 | tf_op jit(solution)/shard_map/ppermute | solution.py:20
  33.1 6.1 %collective-permute-done.kv_ref = bf16[1024,256]{1,0:T(8,128)(2,1)S(1)} collective-permute-done((bf16[1024,256]{1,0:T(8,128)(2,1)S(1)}, bf16[1024,256]{1,0:T(8,128)(2,1)S(1)}, u32[]{:S(2)}, u32[]{:S(2)}) %collective-permute-start) | collective-permute-done | bytes 524320 | tf_op jit(solution)/shard_map/ppermute | solution.py:20
  39.2 0.0 copy-start.3
  39.2 5.6 %collective-permute-start.1 = (bf16[1024,256]{1,0:T(8,128)(2,1)S(1)}, bf16[1024,256]{1,0:T(8,128)(2,1)S(1)}, u32[]{:S(2)}, u32[]{:S(2)}) collective-permute-start(bf16[1024,256]{1,0:T(8,128)(2,1)S(1)} %collective-permute-done.kv_ref), channel_id=1, source_target_pairs={{0,8},{8,16},{16,24},{24,32},{32,40},{40,48},{48,56},{56,64},{64,7... | collective-permute-start | bytes 1572872 | tf_op jit(solution)/shard_map/ppermute | solution.py:20
  44.8 6.1 %collective-permute-done.1.kv_ref = bf16[1024,256]{1,0:T(8,128)(2,1)S(1)} collective-permute-done((bf16[1024,256]{1,0:T(8,128)(2,1)S(1)}, bf16[1024,256]{1,0:T(8,128)(2,1)S(1)}, u32[]{:S(2)}, u32[]{:S(2)}) %collective-permute-start.1) | collective-permute-done | bytes 524320 | tf_op jit(solution)/shard_map/ppermute | solution.py:20
  50.9 0.0 copy-start.2
  50.9 5.6 %collective-permute-start.2 = (bf16[1024,256]{1,0:T(8,128)(2,1)S(1)}, bf16[1024,256]{1,0:T(8,128)(2,1)S(1)}, u32[]{:S(2)}, u32[]{:S(2)}) collective-permute-start(bf16[1024,256]{1,0:T(8,128)(2,1)S(1)} %collective-permute-done.1.kv_ref), channel_id=1, source_target_pairs={{0,8},{8,16},{16,24},{24,32},{32,40},{40,48},{48,56},{56,64},{64,7... | collective-permute-start | bytes 1572872 | tf_op jit(solution)/shard_map/ppermute | solution.py:20
  56.5 0.0 copy-done.1
  56.5 7.9 %shard_map.37 = (f32[4,1,1024]{2,1,0:T(1,128)}, f32[4,1,1024]{2,1,0:T(1,128)}, f32[4,128,1024]{2,1,0:T(8,128)}) custom-call(s32[1]{0:T(128)} %bitcast.pos_ref, bf16[1024,768]{1,0:T(8,128)(2,1)} %bitcast.25, bf16[1024,768]{1,0:T(8,128)(2,1)} %bitcast.26), custom_call_target="tpu_custom_call" | custom-call | tf_op jit(solution)/shard_map/pallas_call | solution.py:116
  64.4 0.0 copy-done.3
  64.4 10.2 %shard_map.38 = (f32[4,1,1024]{2,1,0:T(1,128)}, f32[4,1,1024]{2,1,0:T(1,128)}, f32[4,128,1024]{2,1,0:T(8,128)}) custom-call(s32[1]{0:T(128)} %bitcast.pos_ref, bf16[1024,768]{1,0:T(8,128)(2,1)} %bitcast.27, bf16[1024,256]{1,0:T(8,128)(2,1)} %copy-done.3, ...), custom_call_target="tpu_custom_call", output_to_operand_aliasing={{0}: (3, {}), {1}: (4, {}), {2}: (5, {})} | custom-call | tf_op jit(solution)/shard_map/pallas_call | solution.py:116
  74.6 0.0 copy-done.2
  74.6 10.2 %shard_map.39 = (f32[4,1,1024]{2,1,0:T(1,128)}, f32[4,1,1024]{2,1,0:T(1,128)}, f32[4,128,1024]{2,1,0:T(8,128)}) custom-call(s32[1]{0:T(128)} %bitcast.pos_ref, bf16[1024,768]{1,0:T(8,128)(2,1)} %bitcast.28, bf16[1024,256]{1,0:T(8,128)(2,1)} %copy-done.2, ...), custom_call_target="tpu_custom_call", output_to_operand_aliasing={{0}: (3, {}), {1}: (4, {}), {2}: (5, {})} | custom-call | tf_op jit(solution)/shard_map/pallas_call | solution.py:116
  84.8 0.0 collective-permute-done.2.kv_ref
  84.8 0.0 copy-start.4
  84.8 0.8 copy-done.4
  85.6 10.5 %shard_map.40 = bf16[1024,512]{1,0:T(8,128)(2,1)} custom-call(s32[1]{0:T(128)} %bitcast.pos_ref, bf16[1024,768]{1,0:T(8,128)(2,1)} %bitcast.29, bf16[1024,256]{1,0:T(8,128)(2,1)} %copy-done.4, f32[4,1,1024]{2,1,0:T(1,128)} %get-tuple-element.20.refs_0_, f32[4,1,1024]{2,1,0:T(1,128)} %get-tuple-element.21.refs_1_, f32[4,128,1024]{2,1,0:T(8,128)} %get-tuple-element.22.refs_2_), custom_call_target="tpu_custom_call" | custom-call | tf_op jit(solution)/shard_map/pallas_call | solution.py:116
  96.1 16.3 %all_to_all.35 = bf16[8,128,512]{2,1,0:T(8,128)(2,1)S(1)} all-to-all(bf16[8,128,512]{2,1,0:T(8,128)(2,1)} %bitcast.32), channel_id=1, replica_groups=mesh['ctx'=32,'uly'=8] {'uly'}, dimensions={0} | all-to-all | bytes 2097152 | tf_op jit(solution)/shard_map/all_to_all | solution.py:142
  112.4 1.1 copy.17
  (1 shorter events, 0.0 us)
Async XLA Ops:
  0.0 1.4 %copy-start = (bf16[128,1024]{1,0:T(8,128)(2,1)S(1)}, bf16[128,1024]{1,0:T(8,128)(2,1)}, u32[]{:S(2)}) copy-start(bf16[128,1024]{1,0:T(8,128)(2,1)} %param.4) | copy-start | bytes 786436
  0.0 1.4 %copy-start.5 = (bf16[128,1024]{1,0:T(8,128)(2,1)S(1)}, bf16[128,1024]{1,0:T(8,128)(2,1)}, u32[]{:S(2)}) copy-start(bf16[128,1024]{1,0:T(8,128)(2,1)} %param.5) | copy-start | bytes 786436
  26.6 29.9 %copy-start.1 = (bf16[128,8,768]{2,0,1:T(8,128)(2,1)}, bf16[128,8,768]{2,0,1:T(8,128)(2,1)S(1)}, u32[]{:S(2)}) copy-start(bf16[128,8,768]{2,0,1:T(8,128)(2,1)S(1)} %all_to_all.34) | copy-start | bytes 4718596
  26.6 12.6 %collective-permute-start = (bf16[1024,256]{1,0:T(8,128)(2,1)S(1)}, bf16[1024,256]{1,0:T(8,128)(2,1)S(1)}, u32[]{:S(2)}, u32[]{:S(2)}) collective-permute-start(bf16[1024,256]{1,0:T(8,128)(2,1)S(1)} %slice.4), channel_id=1, source_target_pairs={{0,8},{8,16},{16,24},{24,32},{32,40},{40,48},{48,56},{56,64},{64,7... | collective-permute-start | bytes 1572872 | tf_op jit(solution)/shard_map/ppermute | solution.py:20
  39.2 25.2 %copy-start.3 = (bf16[1024,256]{1,0:T(8,128)(2,1)}, bf16[1024,256]{1,0:T(8,128)(2,1)S(1)}, u32[]{:S(2)}) copy-start(bf16[1024,256]{1,0:T(8,128)(2,1)S(1)} %collective-permute-done.kv_ref) | copy-start | bytes 1572868
  39.2 11.7 %collective-permute-start.1 = (bf16[1024,256]{1,0:T(8,128)(2,1)S(1)}, bf16[1024,256]{1,0:T(8,128)(2,1)S(1)}, u32[]{:S(2)}, u32[]{:S(2)}) collective-permute-start(bf16[1024,256]{1,0:T(8,128)(2,1)S(1)} %collective-permute-done.kv_ref), channel_id=1, source_target_pairs={{0,8},{8,16},{16,24},{24,32},{32,40},{40,48},{48,56},{56,64},{64,7... | collective-permute-start | bytes 1572872 | tf_op jit(solution)/shard_map/ppermute | solution.py:20
  50.9 23.7 %copy-start.2 = (bf16[1024,256]{1,0:T(8,128)(2,1)}, bf16[1024,256]{1,0:T(8,128)(2,1)S(1)}, u32[]{:S(2)}) copy-start(bf16[1024,256]{1,0:T(8,128)(2,1)S(1)} %collective-permute-done.1.kv_ref) | copy-start | bytes 1572868
  50.9 33.9 %collective-permute-start.2 = (bf16[1024,256]{1,0:T(8,128)(2,1)S(1)}, bf16[1024,256]{1,0:T(8,128)(2,1)S(1)}, u32[]{:S(2)}, u32[]{:S(2)}) collective-permute-start(bf16[1024,256]{1,0:T(8,128)(2,1)S(1)} %collective-permute-done.1.kv_ref), channel_id=1, source_target_pairs={{0,8},{8,16},{16,24},{24,32},{32,40},{40,48},{48,56},{56,64},{64,7... | collective-permute-start | bytes 1572872 | tf_op jit(solution)/shard_map/ppermute | solution.py:20
  84.8 0.8 copy-start.4

commit v4 on v3

--- a/solution.py
+++ b/solution.py
@@ -20,7 +20,9 @@
     return lax.ppermute(block, axis, route)
 
 
-def attend_kernel(pos_ref, q_ref, kv_ref, *refs, block_len, back, first, last):
+def attend_kernel(pos_ref, q_ref, *refs, block_len, backs, first, last):
+    n_kv = len(backs)
+    kv_refs, refs = refs[:n_kv], refs[n_kv:]
     if first:
         o_refs, (m_ref, l_ref, acc_ref) = refs[:-3], refs[-3:]
     else:
@@ -37,7 +39,7 @@
         l_ref[...] = l_in[...]
         acc_ref[...] = acc_in[...]
 
-    def process(start, masked):
+    def process(kv_ref, start, masked):
         q = q_ref[...]
         k = kv_ref[pl.ds(start, tile), pl.ds(0, HEAD_SIZE)]
         v = kv_ref[pl.ds(start, tile), pl.ds(HEAD_SIZE, HEAD_SIZE)]
@@ -57,14 +59,15 @@
         acc_ref[...] = acc_ref[...] * factor + pv
         m_ref[...] = m_new
 
-    if back == 0:
-        for t in range(block_len // tile):
-            process(t * tile, True)
-    else:
-        @pl.when(cycle_pos >= back)
-        def _():
+    for back, kv_ref in zip(backs, kv_refs):
+        if back == 0:
             for t in range(block_len // tile):
-                process(t * tile, False)
+                process(kv_ref, t * tile, True)
+        else:
+            @pl.when(cycle_pos >= back)
+            def _():
+                for t in range(block_len // tile):
+                    process(kv_ref, t * tile, False)
 
     if last:
         o_refs[0][...] = (acc_ref[...] / l_ref[...]).T.astype(o_refs[0].dtype)
@@ -74,34 +77,33 @@
         o_refs[2][...] = acc_ref[...]
 
 
-def attend(pos, qkv, kv, carry, q_heads, back, kv_col):
-    block_len = qkv.shape[0]
+def attend(pos, q_src, q_heads, kvs, carry, backs, last):
+    block_len = q_src.shape[0]
     first = carry is None
-    last = back == WINDOW_BLOCKS
-    kernel = functools.partial(attend_kernel, block_len=block_len, back=back, first=first, last=last)
+    kernel = functools.partial(attend_kernel, block_len=block_len, backs=backs, first=first, last=last)
     row_spec = pl.BlockSpec((None, 1, block_len), lambda h, pos: (h, 0, 0))
     acc_spec = pl.BlockSpec((None, HEAD_SIZE, block_len), lambda h, pos: (h, 0, 0))
-    in_specs = [
-        pl.BlockSpec((block_len, HEAD_SIZE), lambda h, pos: (0, h)),
-        pl.BlockSpec((block_len, 2 * HEAD_SIZE), lambda h, pos: (0, kv_col)),
-    ]
-    operands = [pos, qkv, kv]
+    in_specs = [pl.BlockSpec((block_len, HEAD_SIZE), lambda h, pos: (0, h))]
+    operands = [pos, q_src]
+    for kv, col in kvs:
+        in_specs.append(pl.BlockSpec((block_len, 2 * HEAD_SIZE), lambda h, pos, col=col: (0, col)))
+        operands.append(kv)
     if not first:
         in_specs += [row_spec, row_spec, acc_spec]
         operands += list(carry)
-    carry_shapes = [
-        jax.ShapeDtypeStruct((q_heads, 1, block_len), jnp.float32),
-        jax.ShapeDtypeStruct((q_heads, 1, block_len), jnp.float32),
-        jax.ShapeDtypeStruct((q_heads, HEAD_SIZE, block_len), jnp.float32),
-    ]
     if last:
         out_specs = [pl.BlockSpec((block_len, HEAD_SIZE), lambda h, pos: (0, h))]
         out_shape = [jax.ShapeDtypeStruct((block_len, q_heads * HEAD_SIZE), jnp.bfloat16)]
         aliases = {}
     else:
         out_specs = [row_spec, row_spec, acc_spec]
-        out_shape = carry_shapes
-        aliases = {} if first else {3: 0, 4: 1, 5: 2}
+        out_shape = [
+            jax.ShapeDtypeStruct((q_heads, 1, block_len), jnp.float32),
+            jax.ShapeDtypeStruct((q_heads, 1, block_len), jnp.float32),
+            jax.ShapeDtypeStruct((q_heads, HEAD_SIZE, block_len), jnp.float32),
+        ]
+        base = 2 + len(kvs)
+        aliases = {} if first else {base: 0, base + 1: 1, base + 2: 2}
     grid_spec = pltpu.PrefetchScalarGridSpec(
         num_scalar_prefetch=1,
         grid=(q_heads,),
@@ -127,19 +129,39 @@
     n = lax.axis_size("uly")
     rows = queries.shape[0]
     cycle_pos = lax.axis_index("ctx")
+    pos = jnp.reshape(cycle_pos, (1,)).astype(jnp.int32)
+    q_heads = queries.shape[1] // n // HEAD_SIZE
+    half = q_heads // 2
+    q_split = queries.reshape(rows, n, q_heads, HEAD_SIZE)
     packed = jnp.concatenate(
-        [queries.reshape(rows, n, -1), keys.reshape(rows, n, -1), values.reshape(rows, n, -1)], axis=2
+        [
+            q_split[:, :, :half].reshape(rows, n, -1),
+            keys.reshape(rows, n, -1),
+            values.reshape(rows, n, -1),
+        ],
+        axis=2,
     )
     qkv = lax.all_to_all(packed, "uly", split_axis=1, concat_axis=0, tiled=True)
     qkv = qkv.reshape(rows * n, -1)
-    q_heads = (qkv.shape[1] - 2 * HEAD_SIZE) // HEAD_SIZE
-    pos = jnp.reshape(cycle_pos, (1,)).astype(jnp.int32)
-    kv = qkv[:, q_heads * HEAD_SIZE:]
-    carry = attend(pos, qkv, qkv, None, q_heads, 0, q_heads // 2)
+    q_rest = lax.all_to_all(
+        q_split[:, :, half:].reshape(rows, n, -1), "uly", split_axis=1, concat_axis=0, tiled=True
+    )
+    q_rest = q_rest.reshape(rows * n, -1)
+    kv_col = half // 2
+    kv = qkv[:, half * HEAD_SIZE:]
+    blocks = [(qkv, kv_col)]
+    carry = attend(pos, qkv, half, [(qkv, kv_col)], None, (0,), False)
     for back in range(1, WINDOW_BLOCKS + 1):
         kv = passed_along(kv, "ctx", 1)
-        carry = attend(pos, qkv, kv, carry, q_heads, back, 0)
-    return lax.all_to_all(carry, "uly", split_axis=0, concat_axis=1, tiled=True)
+        blocks.append((kv, 0))
+        carry = attend(pos, qkv, half, [(kv, 0)], carry, (back,), back == WINDOW_BLOCKS)
+    out_front = lax.all_to_all(carry, "uly", split_axis=0, concat_axis=1, tiled=True)
+    out_rest = attend(pos, q_rest, q_heads - half, blocks, None, tuple(range(WINDOW_BLOCKS + 1)), True)
+    out_rest = lax.all_to_all(out_rest, "uly", split_axis=0, concat_axis=1, tiled=True)
+    width = half * HEAD_SIZE
+    return jnp.concatenate(
+        [out_front.reshape(rows, n, width), out_rest.reshape(rows, n, width)], axis=2
+    ).reshape(rows, -1)
 
 
 def solution(mesh):

time: 114 us -> 121 us (1.061)
  the two profiles are of different devices: /device:TPU:97 before, /device:TPU:16 now
where the time goes in v4:
time: 121 us; the launch traced here: 120 us
  Pallas kernels  40.8 us (34%)
  blocking collectives  34.2 us (28%)
  waiting for transfers between devices  24.4 us (20%)
  starting transfers between devices  14.8 us (12%)
  local copies, waits for them, and re-layouts  5.96 us (5%)
    pallas_call x5, Pallas kernels, attend(): pl.pallas_call(kernel, grid_spec=grid_spec, out_shape=out_shape, input_ou...  40.8 us
    ppermute x3, waiting for transfers between devices, passed_along(): return lax.ppermute(block, axis, route)  24.4 us
    all_to_all x1, blocking collectives, on_device(): qkv = lax.all_to_all(packed, 'uly', split_axis=1, concat_axis=0, tiled=True)  20.2 us
    all_to_all x1, blocking collectives, on_device(): lax.all_to_all(out_rest, 'uly', split_axis=0, concat_axis=1, tiled=True)  14 us
    ppermute x3, starting transfers between devices, passed_along(): return lax.ppermute(block, axis, route)  5.74 us
    all_to_all x1, starting transfers between devices, on_device(): lax.all_to_all(carry, 'uly', split_axis=0, concat_axis=1, tiled=True)  5.62 us
    all_to_all x1, starting transfers between devices, on_device(): lax.all_to_all(q_split[:, :, half:].reshape(rows, n, -1), 'uly', split_ax...  3.49 us
  transfers between devices with their start and end apart: 5, of which 2 were waited for; matrix products, arithmetic and copies ran while one was open for 1% of the time, Pallas kernels for 34%

profile of v4, /device:TPU:16, one launch (start us, length us, event | category | flops | bytes accessed | tf_op | source)
XLA Modules:
  0.0 120.5 jit_solution(3878437969769862205)
XLA Ops:
  0.0 0.0 copy-start
  0.0 1.8 %reshape.40 = bf16[128,8,4,128]{3,2,1,0:T(4,128)(2,1)S(1)} reshape(bf16[128,4096]{1,0:T(8,128)(2,1)} %param.3) | data formatting | bytes 2097152 | tf_op jit(solution)/shard_map/reshape | solution.py:135
  1.8 0.7 fusion
  2.6 0.0 copy-start.5
  2.6 0.3 reshape.48
  2.9 0.1 copy.15
  3.0 0.0 copy-done
  3.0 0.5 copy-done.5
  3.5 0.1 copy_bitcast_fusion
  3.7 0.1 pad_maximum_fusion
  3.8 20.2 %all_to_all.62 = bf16[128,8,512]{2,0,1:T(8,128)(2,1)S(1)} all-to-all(bf16[128,8,512]{2,0,1:T(8,128)(2,1)S(1)} %pad_maximum_fusion), channel_id=1, replica_groups=mesh['ctx'=32,'uly'=8] {'uly'}, dimensions={1} | all-to-all | bytes 2097152 | tf_op jit(solution)/shard_map/all_to_all | solution.py:144
  23.9 0.0 copy-start.1
  24.0 1.9 %collective-permute-start = (bf16[1024,256]{1,0:T(8,128)(2,1)S(1)}, bf16[1024,256]{1,0:T(8,128)(2,1)S(1)}, u32[]{:S(2)}, u32[]{:S(2)}) collective-permute-start(bf16[1024,256]{1,0:T(8,128)(2,1)S(1)} %slice.13), channel_id=1, source_target_pairs={{0,8},{8,16},{16,24},{24,32},{32,40},{40,48},{48,56},{56,64},{64,7... | collective-permute-start | bytes 1572872 | tf_op jit(solution)/shard_map/ppermute | solution.py:20
  25.9 12.2 %collective-permute-done.refs_0_.refs_1_ = bf16[1024,256]{1,0:T(8,128)(2,1)S(1)} collective-permute-done((bf16[1024,256]{1,0:T(8,128)(2,1)S(1)}, bf16[1024,256]{1,0:T(8,128)(2,1)S(1)}, u32[]{:S(2)}, u32[]{:S(2)}) %collective-permute-start) | collective-permute-done | bytes 524320 | tf_op jit(solution)/shard_map/ppermute | solution.py:20
  38.1 0.0 copy-start.3
  38.1 1.9 %collective-permute-start.1 = (bf16[1024,256]{1,0:T(8,128)(2,1)S(1)}, bf16[1024,256]{1,0:T(8,128)(2,1)S(1)}, u32[]{:S(2)}, u32[]{:S(2)}) collective-permute-start(bf16[1024,256]{1,0:T(8,128)(2,1)S(1)} %collective-permute-done.refs_0_.refs_1_), channel_id=1, source_target_pairs={{0,8},{8,16},{16,24},{24,32},{32,40},{40,48},{48,56},{56,64},{64,7... | collective-permute-start | bytes 1572872 | tf_op jit(solution)/shard_map/ppermute | solution.py:20
  40.0 12.2 %collective-permute-done.1.refs_0_.refs_2_ = bf16[1024,256]{1,0:T(8,128)(2,1)S(1)} collective-permute-done((bf16[1024,256]{1,0:T(8,128)(2,1)S(1)}, bf16[1024,256]{1,0:T(8,128)(2,1)S(1)}, u32[]{:S(2)}, u32[]{:S(2)}) %collective-permute-start.1) | collective-permute-done | bytes 524320 | tf_op jit(solution)/shard_map/ppermute | solution.py:20
  52.2 0.0 copy-start.4
  52.2 1.9 %collective-permute-start.2 = (bf16[1024,256]{1,0:T(8,128)(2,1)S(1)}, bf16[1024,256]{1,0:T(8,128)(2,1)}, u32[]{:S(2)}, u32[]{:S(2)}) collective-permute-start(bf16[1024,256]{1,0:T(8,128)(2,1)S(1)} %collective-permute-done.1.refs_0_.refs_2_), channel_id=1, source_target_pairs={{0,8},{8,16},{16,24},{24,32},{32,40},{40,48},{48,56},{56,64},{64,7... | collective-permute-start | bytes 1572872 | tf_op jit(solution)/shard_map/ppermute | solution.py:20
  54.1 0.3 reshape.49
  54.5 0.0 copy-done.1
  54.5 0.9 copy.16
  55.4 0.0 copy-done.3
  55.4 0.0 copy-done.4
  55.4 3.5 %all-to-all-start.2 = ((bf16[128,8,256]{2,0,1:T(8,128)(2,1)}), bf16[128,8,256]{2,0,1:T(8,128)(2,1)S(1)}, u32[]{:S(2)}, u32[]{:S(2)}) async-start(bf16[128,8,256]{2,0,1:T(8,128)(2,1)} %copy.16), calls=%async_computation.2 | async-start | bytes 1048576 | tf_op jit(solution)/shard_map/all_to_all | solution.py:146
  58.9 4.9 %shard_map.37 = (f32[2,1,1024]{2,1,0:T(1,128)}, f32[2,1,1024]{2,1,0:T(1,128)}, f32[2,128,1024]{2,1,0:T(8,128)}) custom-call(s32[1]{0:T(128)} %bitcast.pos_ref, bf16[1024,512]{1,0:T(8,128)(2,1)} %bitcast.29, bf16[1024,512]{1,0:T(8,128)(2,1)} %bitcast.30), custom_call_target="tpu_custom_call" | custom-call | tf_op jit(solution)/shard_map/pallas_call | solution.py:118
  63.8 6.2 %shard_map.38 = (f32[2,1,1024]{2,1,0:T(1,128)}, f32[2,1,1024]{2,1,0:T(1,128)}, f32[2,128,1024]{2,1,0:T(8,128)}) custom-call(s32[1]{0:T(128)} %bitcast.pos_ref, bf16[1024,512]{1,0:T(8,128)(2,1)} %bitcast.31, bf16[1024,256]{1,0:T(8,128)(2,1)} %copy-done.3, ...), custom_call_target="tpu_custom_call", output_to_operand_aliasing={{0}: (3, {}), {1}: (4, {}), {2}: (5, {})} | custom-call | tf_op jit(solution)/shard_map/pallas_call | solution.py:118
  70.0 6.2 %shard_map.39 = (f32[2,1,1024]{2,1,0:T(1,128)}, f32[2,1,1024]{2,1,0:T(1,128)}, f32[2,128,1024]{2,1,0:T(8,128)}) custom-call(s32[1]{0:T(128)} %bitcast.pos_ref, bf16[1024,512]{1,0:T(8,128)(2,1)} %bitcast.32, bf16[1024,256]{1,0:T(8,128)(2,1)} %copy-done.4, ...), custom_call_target="tpu_custom_call", output_to_operand_aliasing={{0}: (3, {}), {1}: (4, {}), {2}: (5, {})} | custom-call | tf_op jit(solution)/shard_map/pallas_call | solution.py:118
  76.2 0.0 collective-permute-done.2.refs_0_.refs_3_
  76.2 6.4 %shard_map.40 = bf16[1024,256]{1,0:T(8,128)(2,1)} custom-call(s32[1]{0:T(128)} %bitcast.pos_ref, bf16[1024,512]{1,0:T(8,128)(2,1)} %bitcast.33, bf16[1024,256]{1,0:T(8,128)(2,1)} %collective-permute-done.2.refs_0_.refs_3_, f32[2,1,1024]{2,1,0:T(1,128)} %get-tuple-element.20.refs_1_, f32[2,1,1024]{2,1,0:T(1,128)} %get-tuple-element.21.refs_2_, ...), custom_call_target="tpu_custom_call" | custom-call | tf_op jit(solution)/shard_map/pallas_call | solution.py:118
  82.6 0.0 all-to-all-done.2
  82.6 0.0 copy-start.2
  82.6 5.6 %all-to-all-start.1 = ((bf16[8,128,256]{2,1,0:T(8,128)(2,1)}), bf16[8,128,256]{2,1,0:T(8,128)(2,1)S(1)}, u32[]{:S(2)}, u32[]{:S(2)}) async-start(bf16[8,128,256]{2,1,0:T(8,128)(2,1)} %bitcast.36), calls=%async_computation.1 | async-start | bytes 1048576 | tf_op jit(solution)/shard_map/all_to_all | solution.py:158
  88.2 0.0 copy-done.2
  88.2 17.1 %shard_map.41 = bf16[1024,256]{1,0:T(8,128)(2,1)} custom-call(s32[1]{0:T(128)} %bitcast.pos_ref, bf16[1024,256]{1,0:T(8,128)(2,1)} %bitcast.35, bf16[1024,512]{1,0:T(8,128)(2,1)} %bitcast.34, bf16[1024,256]{1,0:T(8,128)(2,1)} %copy-done.3, bf16[1024,256]{1,0:T(8,128)(2,1)} %copy-done.4, bf16[1024,256]{1,0:T(8,128)(2,1)} %collective-permute-done.2.refs_0_.refs_3_), custom_call_target="tpu_custom_call" | custom-call | tf_op jit(solution)/shard_map/pallas_call | solution.py:118
  105.3 0.0 all-to-all-done.1
  105.3 14.0 %all_to_all.63 = bf16[8,128,256]{2,1,0:T(8,128)(2,1)S(1)} all-to-all(bf16[8,128,256]{2,1,0:T(8,128)(2,1)} %bitcast.38), channel_id=1, replica_groups=mesh['ctx'=32,'uly'=8] {'uly'}, dimensions={0} | all-to-all | bytes 1048576 | tf_op jit(solution)/shard_map/all_to_all | solution.py:160
  119.3 0.1 maximum_bitcast_fusion
  119.4 1.1 copy.19
  (1 shorter events, 0.0 us)
Async XLA Ops:
  0.0 3.0 %copy-start = (bf16[128,1024]{1,0:T(8,128)(2,1)S(1)}, bf16[128,1024]{1,0:T(8,128)(2,1)}, u32[]{:S(2)}) copy-start(bf16[128,1024]{1,0:T(8,128)(2,1)} %param.4) | copy-start | bytes 786436
  2.6 1.0 copy-start.5
  23.9 30.5 %copy-start.1 = (bf16[128,8,512]{2,0,1:T(8,128)(2,1)}, bf16[128,8,512]{2,0,1:T(8,128)(2,1)S(1)}, u32[]{:S(2)}) copy-start(bf16[128,8,512]{2,0,1:T(8,128)(2,1)S(1)} %all_to_all.62) | copy-start | bytes 3145732
  24.0 14.1 %collective-permute-start = (bf16[1024,256]{1,0:T(8,128)(2,1)S(1)}, bf16[1024,256]{1,0:T(8,128)(2,1)S(1)}, u32[]{:S(2)}, u32[]{:S(2)}) collective-permute-start(bf16[1024,256]{1,0:T(8,128)(2,1)S(1)} %slice.13), channel_id=1, source_target_pairs={{0,8},{8,16},{16,24},{24,32},{32,40},{40,48},{48,56},{56,64},{64,7... | collective-permute-start | bytes 1572872 | tf_op jit(solution)/shard_map/ppermute | solution.py:20
  38.1 17.3 %copy-start.3 = (bf16[1024,256]{1,0:T(8,128)(2,1)}, bf16[1024,256]{1,0:T(8,128)(2,1)S(1)}, u32[]{:S(2)}) copy-start(bf16[1024,256]{1,0:T(8,128)(2,1)S(1)} %collective-permute-done.refs_0_.refs_1_) | copy-start | bytes 1572868
  38.1 14.1 %collective-permute-start.1 = (bf16[1024,256]{1,0:T(8,128)(2,1)S(1)}, bf16[1024,256]{1,0:T(8,128)(2,1)S(1)}, u32[]{:S(2)}, u32[]{:S(2)}) collective-permute-start(bf16[1024,256]{1,0:T(8,128)(2,1)S(1)} %collective-permute-done.refs_0_.refs_1_), channel_id=1, source_target_pairs={{0,8},{8,16},{16,24},{24,32},{32,40},{40,48},{48,56},{56,64},{64,7... | collective-permute-start | bytes 1572872 | tf_op jit(solution)/shard_map/ppermute | solution.py:20
  52.2 3.2 %copy-start.4 = (bf16[1024,256]{1,0:T(8,128)(2,1)}, bf16[1024,256]{1,0:T(8,128)(2,1)S(1)}, u32[]{:S(2)}) copy-start(bf16[1024,256]{1,0:T(8,128)(2,1)S(1)} %collective-permute-done.1.refs_0_.refs_2_) | copy-start | bytes 1572868
  52.2 24.0 %collective-permute-start.2 = (bf16[1024,256]{1,0:T(8,128)(2,1)S(1)}, bf16[1024,256]{1,0:T(8,128)(2,1)}, u32[]{:S(2)}, u32[]{:S(2)}) collective-permute-start(bf16[1024,256]{1,0:T(8,128)(2,1)S(1)} %collective-permute-done.1.refs_0_.refs_2_), channel_id=1, source_target_pairs={{0,8},{8,16},{16,24},{24,32},{32,40},{40,48},{48,56},{56,64},{64,7... | collective-permute-start | bytes 1572872 | tf_op jit(solution)/shard_map/ppermute | solution.py:20
  55.4 27.2 %all-to-all-start.2 = ((bf16[128,8,256]{2,0,1:T(8,128)(2,1)}), bf16[128,8,256]{2,0,1:T(8,128)(2,1)S(1)}, u32[]{:S(2)}, u32[]{:S(2)}) async-start(bf16[128,8,256]{2,0,1:T(8,128)(2,1)} %copy.16), calls=%async_computation.2 | async-start | bytes 1048576 | tf_op jit(solution)/shard_map/all_to_all | solution.py:146
  82.6 5.6 %copy-start.2 = (bf16[128,8,256]{2,0,1:T(8,128)(2,1)}, bf16[128,8,256]{2,0,1:T(8,128)(2,1)S(1)}, u32[]{:S(2)}) copy-start(bf16[128,8,256]{2,0,1:T(8,128)(2,1)S(1)} %all-to-all-done.2) | copy-start | bytes 1572868
  82.6 22.7 %all-to-all-start.1 = ((bf16[8,128,256]{2,1,0:T(8,128)(2,1)}), bf16[8,128,256]{2,1,0:T(8,128)(2,1)S(1)}, u32[]{:S(2)}, u32[]{:S(2)}) async-start(bf16[8,128,256]{2,1,0:T(8,128)(2,1)} %bitcast.36), calls=%async_computation.1 | async-start | bytes 1048576 | tf_op jit(solution)/shard_map/all_to_all | solution.py:158

commit v5 on v3

--- a/solution.py
+++ b/solution.py
@@ -37,7 +37,7 @@
         l_ref[...] = l_in[...]
         acc_ref[...] = acc_in[...]
 
-    def process(start, masked):
+    def process(start, masked, visible=None):
         q = q_ref[...]
         k = kv_ref[pl.ds(start, tile), pl.ds(0, HEAD_SIZE)]
         v = kv_ref[pl.ds(start, tile), pl.ds(HEAD_SIZE, HEAD_SIZE)]
@@ -46,6 +46,8 @@
             keys = lax.broadcasted_iota(jnp.int32, s.shape, 0) + start
             rows = lax.broadcasted_iota(jnp.int32, s.shape, 1)
             s = jnp.where(keys <= rows, s, jnp.float32(-1e30))
+        if visible is not None:
+            s = jnp.where(visible, s, -jnp.inf)
         m_old = m_ref[...]
         m_new = jnp.maximum(m_old, jnp.max(s, axis=0, keepdims=True))
         p = jnp.exp2((s - m_new) * exp_scale)
@@ -61,10 +63,8 @@
         for t in range(block_len // tile):
             process(t * tile, True)
     else:
-        @pl.when(cycle_pos >= back)
-        def _():
-            for t in range(block_len // tile):
-                process(t * tile, False)
+        for t in range(block_len // tile):
+            process(t * tile, False, cycle_pos >= back)
 
     if last:
         o_refs[0][...] = (acc_ref[...] / l_ref[...]).T.astype(o_refs[0].dtype)

time: 114 us -> 115 us (level)
  no operation moved by 1% of the time
where the time goes in v5:
time: 115 us
  blocking collectives  41.3 us (36%)
  Pallas kernels  39.8 us (35%)
  starting transfers between devices  17.7 us (15%)
  waiting for transfers between devices  12.2 us (11%)
  local copies, waits for them, and re-layouts  3.4 us (3%)
    pallas_call x4, Pallas kernels, attend(): pl.pallas_call(kernel, grid_spec=grid_spec, out_shape=out_shape, input_ou...  39.8 us
    all_to_all x1, blocking collectives, on_device(): qkv = lax.all_to_all(packed, 'uly', split_axis=1, concat_axis=0, tiled=True)  24.9 us
    ppermute x3, starting transfers between devices, passed_along(): return lax.ppermute(block, axis, route)  17.7 us
    all_to_all x1, blocking collectives, on_device(): return lax.all_to_all(carry, 'uly', split_axis=0, concat_axis=1, tiled=True)  16.4 us
    ppermute x3, waiting for transfers between devices, passed_along(): return lax.ppermute(block, axis, route)  12.2 us
  transfers between devices with their start and end apart: 3, of which 2 were waited for; matrix products, arithmetic and copies ran while one was open for 0% of the time, Pallas kernels for 25%

profile of v5, /device:TPU:97, one launch (start us, length us, event | category | flops | bytes accessed | tf_op | source)
XLA Modules:
  0.0 114.5 jit_solution(4412777105236601897)
XLA Ops:
  0.0 0.0 copy-start
  0.0 0.0 copy-start.5
  0.0 1.4 %copy.21 = bf16[16,8,8,512]{3,2,0,1:T(8,128)(2,1)S(1)} copy(bf16[16,8,8,512]{3,2,1,0:T(8,128)(2,1)} %bitcast.33) | data formatting | bytes 2097152 | tf_op jit(solution)/shard_map/reshape | solution.py:131
  1.4 0.0 copy-done
  1.4 0.0 copy-done.5
  1.4 0.1 copy_bitcast_fusion.1
  1.5 0.1 pad_maximum_fusion
  1.7 24.9 %all_to_all.34 = bf16[128,8,768]{2,0,1:T(8,128)(2,1)S(1)} all-to-all(bf16[128,8,768]{2,0,1:T(8,128)(2,1)S(1)} %pad_maximum_fusion), channel_id=1, replica_groups=mesh['ctx'=32,'uly'=8] {'uly'}, dimensions={1} | all-to-all | bytes 3145728 | tf_op jit(solution)/shard_map/all_to_all | solution.py:133
  26.6 0.0 copy-start.1
  26.6 6.5 %collective-permute-start = (bf16[1024,256]{1,0:T(8,128)(2,1)S(1)}, bf16[1024,256]{1,0:T(8,128)(2,1)S(1)}, u32[]{:S(2)}, u32[]{:S(2)}) collective-permute-start(bf16[1024,256]{1,0:T(8,128)(2,1)S(1)} %slice.4), channel_id=1, source_target_pairs={{0,8},{8,16},{16,24},{24,32},{32,40},{40,48},{48,56},{56,64},{64,7... | collective-permute-start | bytes 1572872 | tf_op jit(solution)/shard_map/ppermute | solution.py:20
  33.1 6.1 %collective-permute-done.kv_ref = bf16[1024,256]{1,0:T(8,128)(2,1)S(1)} collective-permute-done((bf16[1024,256]{1,0:T(8,128)(2,1)S(1)}, bf16[1024,256]{1,0:T(8,128)(2,1)S(1)}, u32[]{:S(2)}, u32[]{:S(2)}) %collective-permute-start) | collective-permute-done | bytes 524320 | tf_op jit(solution)/shard_map/ppermute | solution.py:20
  39.2 0.0 copy-start.3
  39.2 5.6 %collective-permute-start.1 = (bf16[1024,256]{1,0:T(8,128)(2,1)S(1)}, bf16[1024,256]{1,0:T(8,128)(2,1)S(1)}, u32[]{:S(2)}, u32[]{:S(2)}) collective-permute-start(bf16[1024,256]{1,0:T(8,128)(2,1)S(1)} %collective-permute-done.kv_ref), channel_id=1, source_target_pairs={{0,8},{8,16},{16,24},{24,32},{32,40},{40,48},{48,56},{56,64},{64,7... | collective-permute-start | bytes 1572872 | tf_op jit(solution)/shard_map/ppermute | solution.py:20
  44.8 6.1 %collective-permute-done.1.kv_ref = bf16[1024,256]{1,0:T(8,128)(2,1)S(1)} collective-permute-done((bf16[1024,256]{1,0:T(8,128)(2,1)S(1)}, bf16[1024,256]{1,0:T(8,128)(2,1)S(1)}, u32[]{:S(2)}, u32[]{:S(2)}) %collective-permute-start.1) | collective-permute-done | bytes 524320 | tf_op jit(solution)/shard_map/ppermute | solution.py:20
  50.9 0.0 copy-start.2
  50.9 5.6 %collective-permute-start.2 = (bf16[1024,256]{1,0:T(8,128)(2,1)S(1)}, bf16[1024,256]{1,0:T(8,128)(2,1)S(1)}, u32[]{:S(2)}, u32[]{:S(2)}) collective-permute-start(bf16[1024,256]{1,0:T(8,128)(2,1)S(1)} %collective-permute-done.1.kv_ref), channel_id=1, source_target_pairs={{0,8},{8,16},{16,24},{24,32},{32,40},{40,48},{48,56},{56,64},{64,7... | collective-permute-start | bytes 1572872 | tf_op jit(solution)/shard_map/ppermute | solution.py:20
  56.5 0.0 copy-done.1
  56.5 7.9 %shard_map.37 = (f32[4,1,1024]{2,1,0:T(1,128)}, f32[4,1,1024]{2,1,0:T(1,128)}, f32[4,128,1024]{2,1,0:T(8,128)}) custom-call(s32[1]{0:T(128)} %bitcast.pos_ref, bf16[1024,768]{1,0:T(8,128)(2,1)} %bitcast.25, bf16[1024,768]{1,0:T(8,128)(2,1)} %bitcast.26), custom_call_target="tpu_custom_call" | custom-call | tf_op jit(solution)/shard_map/pallas_call | solution.py:116
  64.4 0.0 copy-done.3
  64.4 10.6 %shard_map.38 = (f32[4,1,1024]{2,1,0:T(1,128)}, f32[4,1,1024]{2,1,0:T(1,128)}, f32[4,128,1024]{2,1,0:T(8,128)}) custom-call(s32[1]{0:T(128)} %bitcast.pos_ref, bf16[1024,768]{1,0:T(8,128)(2,1)} %bitcast.27, bf16[1024,256]{1,0:T(8,128)(2,1)} %copy-done.3, ...), custom_call_target="tpu_custom_call", output_to_operand_aliasing={{0}: (3, {}), {1}: (4, {}), {2}: (5, {})} | custom-call | tf_op jit(solution)/shard_map/pallas_call | solution.py:116
  75.0 0.0 copy-done.2
  75.0 10.6 %shard_map.39 = (f32[4,1,1024]{2,1,0:T(1,128)}, f32[4,1,1024]{2,1,0:T(1,128)}, f32[4,128,1024]{2,1,0:T(8,128)}) custom-call(s32[1]{0:T(128)} %bitcast.pos_ref, bf16[1024,768]{1,0:T(8,128)(2,1)} %bitcast.28, bf16[1024,256]{1,0:T(8,128)(2,1)} %copy-done.2, ...), custom_call_target="tpu_custom_call", output_to_operand_aliasing={{0}: (3, {}), {1}: (4, {}), {2}: (5, {})} | custom-call | tf_op jit(solution)/shard_map/pallas_call | solution.py:116
  85.6 0.0 collective-permute-done.2.kv_ref
  85.6 0.0 copy-start.4
  85.6 0.8 copy-done.4
  86.4 10.7 %shard_map.40 = bf16[1024,512]{1,0:T(8,128)(2,1)} custom-call(s32[1]{0:T(128)} %bitcast.pos_ref, bf16[1024,768]{1,0:T(8,128)(2,1)} %bitcast.29, bf16[1024,256]{1,0:T(8,128)(2,1)} %copy-done.4, f32[4,1,1024]{2,1,0:T(1,128)} %get-tuple-element.20.refs_0_, f32[4,1,1024]{2,1,0:T(1,128)} %get-tuple-element.21.refs_1_, f32[4,128,1024]{2,1,0:T(8,128)} %get-tuple-element.22.refs_2_), custom_call_target="tpu_custom_call" | custom-call | tf_op jit(solution)/shard_map/pallas_call | solution.py:116
  97.1 16.4 %all_to_all.35 = bf16[8,128,512]{2,1,0:T(8,128)(2,1)S(1)} all-to-all(bf16[8,128,512]{2,1,0:T(8,128)(2,1)} %bitcast.32), channel_id=1, replica_groups=mesh['ctx'=32,'uly'=8] {'uly'}, dimensions={0} | all-to-all | bytes 2097152 | tf_op jit(solution)/shard_map/all_to_all | solution.py:142
  113.5 1.1 copy.17
  (1 shorter events, 0.0 us)
Async XLA Ops:
  0.0 1.4 %copy-start = (bf16[128,1024]{1,0:T(8,128)(2,1)S(1)}, bf16[128,1024]{1,0:T(8,128)(2,1)}, u32[]{:S(2)}) copy-start(bf16[128,1024]{1,0:T(8,128)(2,1)} %param.4) | copy-start | bytes 786436
  0.0 1.4 %copy-start.5 = (bf16[128,1024]{1,0:T(8,128)(2,1)S(1)}, bf16[128,1024]{1,0:T(8,128)(2,1)}, u32[]{:S(2)}) copy-start(bf16[128,1024]{1,0:T(8,128)(2,1)} %param.5) | copy-start | bytes 786436
  26.6 29.9 %copy-start.1 = (bf16[128,8,768]{2,0,1:T(8,128)(2,1)}, bf16[128,8,768]{2,0,1:T(8,128)(2,1)S(1)}, u32[]{:S(2)}) copy-start(bf16[128,8,768]{2,0,1:T(8,128)(2,1)S(1)} %all_to_all.34) | copy-start | bytes 4718596
  26.6 12.6 %collective-permute-start = (bf16[1024,256]{1,0:T(8,128)(2,1)S(1)}, bf16[1024,256]{1,0:T(8,128)(2,1)S(1)}, u32[]{:S(2)}, u32[]{:S(2)}) collective-permute-start(bf16[1024,256]{1,0:T(8,128)(2,1)S(1)} %slice.4), channel_id=1, source_target_pairs={{0,8},{8,16},{16,24},{24,32},{32,40},{40,48},{48,56},{56,64},{64,7... | collective-permute-start | bytes 1572872 | tf_op jit(solution)/shard_map/ppermute | solution.py:20
  39.2 25.2 %copy-start.3 = (bf16[1024,256]{1,0:T(8,128)(2,1)}, bf16[1024,256]{1,0:T(8,128)(2,1)S(1)}, u32[]{:S(2)}) copy-start(bf16[1024,256]{1,0:T(8,128)(2,1)S(1)} %collective-permute-done.kv_ref) | copy-start | bytes 1572868
  39.2 11.7 %collective-permute-start.1 = (bf16[1024,256]{1,0:T(8,128)(2,1)S(1)}, bf16[1024,256]{1,0:T(8,128)(2,1)S(1)}, u32[]{:S(2)}, u32[]{:S(2)}) collective-permute-start(bf16[1024,256]{1,0:T(8,128)(2,1)S(1)} %collective-permute-done.kv_ref), channel_id=1, source_target_pairs={{0,8},{8,16},{16,24},{24,32},{32,40},{40,48},{48,56},{56,64},{64,7... | collective-permute-start | bytes 1572872 | tf_op jit(solution)/shard_map/ppermute | solution.py:20
  50.9 24.1 %copy-start.2 = (bf16[1024,256]{1,0:T(8,128)(2,1)}, bf16[1024,256]{1,0:T(8,128)(2,1)S(1)}, u32[]{:S(2)}) copy-start(bf16[1024,256]{1,0:T(8,128)(2,1)S(1)} %collective-permute-done.1.kv_ref) | copy-start | bytes 1572868
  50.9 34.7 %collective-permute-start.2 = (bf16[1024,256]{1,0:T(8,128)(2,1)S(1)}, bf16[1024,256]{1,0:T(8,128)(2,1)S(1)}, u32[]{:S(2)}, u32[]{:S(2)}) collective-permute-start(bf16[1024,256]{1,0:T(8,128)(2,1)S(1)} %collective-permute-done.1.kv_ref), channel_id=1, source_target_pairs={{0,8},{8,16},{16,24},{24,32},{32,40},{40,48},{48,56},{56,64},{64,7... | collective-permute-start | bytes 1572872 | tf_op jit(solution)/shard_map/ppermute | solution.py:20
  85.6 0.8 copy-start.4

commit v6 on v3

v6 whole, which is shorter than its diff:
```python
import functools

import jax
import jax.numpy as jnp
from jax import lax
from jax.experimental import pallas as pl
from jax.experimental.pallas import tpu as pltpu
from jax.sharding import PartitionSpec as P


HEAD_SIZE = 128
WINDOW_BLOCKS = 3
KEY_TILE = 1024
LOG2_E = 1.4426950408889634


def passed_along(block, axis, distance):
    devices = range(lax.axis_size(axis))
    route = [(i - distance, i) for i in devices if i - distance in devices]
    return lax.ppermute(block, axis, route)


def attend_kernel(pos_ref, q_ref, kv_ref, *refs, block_len, back, last):
    if last:
        parts = [refs[3 * i:3 * i + 3] for i in range(WINDOW_BLOCKS)]
        o_ref = refs[3 * WINDOW_BLOCKS]
        m_ref, l_ref, acc_ref = refs[3 * WINDOW_BLOCKS + 1:]
    else:
        m_ref, l_ref, acc_ref = refs
    cycle_pos = pos_ref[0]
    exp_scale = HEAD_SIZE ** (-0.5) * LOG2_E
    tile = min(KEY_TILE, block_len)

    def process(start, masked, fresh):
        q = q_ref[...]
        k = kv_ref[pl.ds(start, tile), pl.ds(0, HEAD_SIZE)]
        v = kv_ref[pl.ds(start, tile), pl.ds(HEAD_SIZE, HEAD_SIZE)]
        s = lax.dot_general(k, q, (((1,), (1,)), ((), ())), preferred_element_type=jnp.float32)
        if masked:
            keys = lax.broadcasted_iota(jnp.int32, s.shape, 0) + start
            rows = lax.broadcasted_iota(jnp.int32, s.shape, 1)
            s = jnp.where(keys <= rows, s, jnp.float32(-1e30))
        if fresh:
            m_new = jnp.max(s, axis=0, keepdims=True)
        else:
            m_old = m_ref[...]
            m_new = jnp.maximum(m_old, jnp.max(s, axis=0, keepdims=True))
        p = jnp.exp2((s - m_new) * exp_scale)
        pv = lax.dot_general(
            v, p.astype(jnp.bfloat16), (((0,), (0,)), ((), ())), preferred_element_type=jnp.float32
        )
        if fresh:
            l_ref[...] = jnp.sum(p, axis=0, keepdims=True)
            acc_ref[...] = pv
        else:
            factor = jnp.exp2((m_old - m_new) * exp_scale)
            l_ref[...] = l_ref[...] * factor + jnp.sum(p, axis=0, keepdims=True)
            acc_ref[...] = acc_ref[...] * factor + pv
        m_ref[...] = m_new

    starts = [t * tile for t in range(block_len // tile)]
    if back == 0:
        for j, start in enumerate(starts):
            process(start, True, j == 0)
    else:
        @pl.when(cycle_pos >= back)
        def _():
            for j, start in enumerate(starts):
                process(start, False, j == 0)

        @pl.when(cycle_pos < back)
        def _():
            m_ref[...] = jnp.full(m_ref.shape, -jnp.inf, jnp.float32)
            l_ref[...] = jnp.zeros(l_ref.shape, jnp.float32)
            acc_ref[...] = jnp.zeros(acc_ref.shape, jnp.float32)

    if last:
        states = [(r[0][...], r[1][...], r[2][...]) for r in parts] + [(m_ref[...], l_ref[...], acc_ref[...])]
        m_all = states[0][0]
        for m_b, _, _ in states[1:]:
            m_all = jnp.maximum(m_all, m_b)
        total = jnp.zeros_like(m_all)
        acc = jnp.zeros(acc_ref.shape, jnp.float32)
        for m_b, l_b, acc_b in states:
            factor = jnp.exp2((m_b - m_all) * exp_scale)
            total = total + l_b * factor
            acc = acc + acc_b * factor
        o_ref[...] = (acc / total).T.astype(o_ref.dtype)


def attend(pos, q_src, kv, kv_col, q_heads, back, parts=None):
    block_len = q_src.shape[0]
    last = parts is not None
    kernel = functools.partial(attend_kernel, block_len=block_len, back=back, last=last)
    row_spec = pl.BlockSpec((None, 1, block_len), lambda h, pos: (h, 0, 0))
    acc_spec = pl.BlockSpec((None, HEAD_SIZE, block_len), lambda h, pos: (h, 0, 0))
    in_specs = [
        pl.BlockSpec((block_len, HEAD_SIZE), lambda h, pos: (0, h)),
        pl.BlockSpec((block_len, 2 * HEAD_SIZE), lambda h, pos: (0, kv_col)),
    ]
    operands = [pos, q_src, kv]
    state_shapes = [
        jax.ShapeDtypeStruct((q_heads, 1, block_len), jnp.float32),
        jax.ShapeDtypeStruct((q_heads, 1, block_len), jnp.float32),
        jax.ShapeDtypeStruct((q_heads, HEAD_SIZE, block_len), jnp.float32),
    ]
    if last:
        for part in parts:
            in_specs += [row_spec, row_spec, acc_spec]
            operands += list(part)
        out_specs = pl.BlockSpec((block_len, HEAD_SIZE), lambda h, pos: (0, h))
        out_shape = jax.ShapeDtypeStruct((block_len, q_heads * HEAD_SIZE), jnp.bfloat16)
        scratch = [
            pltpu.VMEM((1, block_len), jnp.float32),
            pltpu.VMEM((1, block_len), jnp.float32),
            pltpu.VMEM((HEAD_SIZE, block_len), jnp.float32),
        ]
    else:
        out_specs = [row_spec, row_spec, acc_spec]
        out_shape = state_shapes
        scratch = []
    grid_spec = pltpu.PrefetchScalarGridSpec(
        num_scalar_prefetch=1,
        grid=(q_heads,),
        in_specs=in_specs,
        out_specs=out_specs,
        scratch_shapes=scratch,
    )
    return pl.pallas_call(
        kernel,
        grid_spec=grid_spec,
        out_shape=out_shape,
        compiler_params=pltpu.CompilerParams(dimension_semantics=("arbitrary",)),
    )(*operands)


def on_device(queries, keys, values):
    n = lax.axis_size("uly")
    rows = queries.shape[0]
    cycle_pos = lax.axis_index("ctx")
    packed = jnp.concatenate(
        [queries.reshape(rows, n, -1), keys.reshape(rows, n, -1), values.reshape(rows, n, -1)], axis=2
    )
    qkv = lax.all_to_all(packed, "uly", split_axis=1, concat_axis=0, tiled=True)
    qkv = qkv.reshape(rows * n, -1)
    q_heads = (qkv.shape[1] - 2 * HEAD_SIZE) // HEAD_SIZE
    pos = jnp.reshape(cycle_pos, (1,)).astype(jnp.int32)
    kv = qkv[:, q_heads * HEAD_SIZE:]
    parts = [attend(pos, qkv, qkv, q_heads // 2, q_heads, 0)]
    for back in range(1, WINDOW_BLOCKS + 1):
        kv = passed_along(kv, "ctx", 1)
        last = back == WINDOW_BLOCKS
        parts.append(attend(pos, qkv, kv, 0, q_heads, back, parts if last else None))
    return lax.all_to_all(parts[-1], "uly", split_axis=0, concat_axis=1, tiled=True)


def solution(mesh):
    placed = (P(("ctx", "uly"), None), P(("ctx", "uly"), None), P(("ctx", "uly"), None))
    return jax.shard_map(
        on_device, mesh=mesh, in_specs=placed, out_specs=P(("ctx", "uly"), None), check_vma=False
    )
```

time: 114 us -> 111 us (0.974)
  Pallas kernels: 38.7 us -> 35.7 us
    pallas_call x4, Pallas kernels: 38.7 us -> 35.7 us  [attend(): pl.pallas_call(kernel, grid_spec=grid_spec, out_shape=out_shape, compiler...]
  transfers between devices with their start and end apart: 3 -> 3, of which waited for: 2 -> 2; matrix products, arithmetic and copies ran while one was open for 0% -> 0% of each run, Pallas kernels for 25% -> 23%
where the time goes in v6:
time: 111 us; the launch traced here: 110 us
  blocking collectives  41.3 us (37%)
  Pallas kernels  35.7 us (32%)
  starting transfers between devices  17.7 us (16%)
  waiting for transfers between devices  12.2 us (11%)
  local copies, waits for them, and re-layouts  3.46 us (3%)
    pallas_call x4, Pallas kernels, attend(): pl.pallas_call(kernel, grid_spec=grid_spec, out_shape=out_shape, compiler...  35.7 us
    all_to_all x1, blocking collectives, on_device(): qkv = lax.all_to_all(packed, 'uly', split_axis=1, concat_axis=0, tiled=True)  24.9 us
    ppermute x3, starting transfers between devices, passed_along(): return lax.ppermute(block, axis, route)  17.7 us
    all_to_all x1, blocking collectives, on_device(): lax.all_to_all(parts[-1], 'uly', split_axis=0, concat_axis=1, tiled=True)  16.4 us
    ppermute x3, waiting for transfers between devices, passed_along(): return lax.ppermute(block, axis, route)  12.2 us
  transfers between devices with their start and end apart: 3, of which 2 were waited for; matrix products, arithmetic and copies ran while one was open for 0% of the time, Pallas kernels for 23%

profile of v6, /device:TPU:97, one launch (start us, length us, event | category | flops | bytes accessed | tf_op | source)
XLA Modules:
  0.0 110.5 jit_solution(11976488931357259355)
XLA Ops:
  0.0 0.0 copy-start
  0.0 0.0 copy-start.5
  0.0 1.4 %copy.15 = bf16[16,8,8,512]{3,2,0,1:T(8,128)(2,1)S(1)} copy(bf16[16,8,8,512]{3,2,1,0:T(8,128)(2,1)} %bitcast.33) | data formatting | bytes 2097152 | tf_op jit(solution)/shard_map/reshape | solution.py:142
  1.4 0.0 copy-done
  1.4 0.0 copy-done.5
  1.4 0.1 copy_bitcast_fusion.1
  1.5 0.1 pad_maximum_fusion
  1.7 24.9 %all_to_all.34 = bf16[128,8,768]{2,0,1:T(8,128)(2,1)S(1)} all-to-all(bf16[128,8,768]{2,0,1:T(8,128)(2,1)S(1)} %pad_maximum_fusion), channel_id=1, replica_groups=mesh['ctx'=32,'uly'=8] {'uly'}, dimensions={1} | all-to-all | bytes 3145728 | tf_op jit(solution)/shard_map/all_to_all | solution.py:144
  26.6 0.0 copy-start.1
  26.6 6.5 %collective-permute-start = (bf16[1024,256]{1,0:T(8,128)(2,1)S(1)}, bf16[1024,256]{1,0:T(8,128)(2,1)S(1)}, u32[]{:S(2)}, u32[]{:S(2)}) collective-permute-start(bf16[1024,256]{1,0:T(8,128)(2,1)S(1)} %slice.4), channel_id=1, source_target_pairs={{0,8},{8,16},{16,24},{24,32},{32,40},{40,48},{48,56},{56,64},{64,7... | collective-permute-start | bytes 1572872 | tf_op jit(solution)/shard_map/ppermute | solution.py:20
  33.1 6.1 %collective-permute-done.kv_ref = bf16[1024,256]{1,0:T(8,128)(2,1)S(1)} collective-permute-done((bf16[1024,256]{1,0:T(8,128)(2,1)S(1)}, bf16[1024,256]{1,0:T(8,128)(2,1)S(1)}, u32[]{:S(2)}, u32[]{:S(2)}) %collective-permute-start) | collective-permute-done | bytes 524320 | tf_op jit(solution)/shard_map/ppermute | solution.py:20
  39.2 0.0 copy-start.2
  39.2 5.6 %collective-permute-start.1 = (bf16[1024,256]{1,0:T(8,128)(2,1)S(1)}, bf16[1024,256]{1,0:T(8,128)(2,1)S(1)}, u32[]{:S(2)}, u32[]{:S(2)}) collective-permute-start(bf16[1024,256]{1,0:T(8,128)(2,1)S(1)} %collective-permute-done.kv_ref), channel_id=1, source_target_pairs={{0,8},{8,16},{16,24},{24,32},{32,40},{40,48},{48,56},{56,64},{64,7... | collective-permute-start | bytes 1572872 | tf_op jit(solution)/shard_map/ppermute | solution.py:20
  44.8 6.1 %collective-permute-done.1.kv_ref = bf16[1024,256]{1,0:T(8,128)(2,1)S(1)} collective-permute-done((bf16[1024,256]{1,0:T(8,128)(2,1)S(1)}, bf16[1024,256]{1,0:T(8,128)(2,1)S(1)}, u32[]{:S(2)}, u32[]{:S(2)}) %collective-permute-start.1) | collective-permute-done | bytes 524320 | tf_op jit(solution)/shard_map/ppermute | solution.py:20
  50.9 0.0 copy-start.4
  50.9 5.6 %collective-permute-start.2 = (bf16[1024,256]{1,0:T(8,128)(2,1)S(1)}, bf16[1024,256]{1,0:T(8,128)(2,1)S(1)}, u32[]{:S(2)}, u32[]{:S(2)}) collective-permute-start(bf16[1024,256]{1,0:T(8,128)(2,1)S(1)} %collective-permute-done.1.kv_ref), channel_id=1, source_target_pairs={{0,8},{8,16},{16,24},{24,32},{32,40},{40,48},{48,56},{56,64},{64,7... | collective-permute-start | bytes 1572872 | tf_op jit(solution)/shard_map/ppermute | solution.py:20
  56.5 0.0 copy-done.1
  56.5 7.0 %shard_map.37 = (f32[4,1,1024]{2,1,0:T(1,128)}, f32[4,1,1024]{2,1,0:T(1,128)}, f32[4,128,1024]{2,1,0:T(8,128)}) custom-call(s32[1]{0:T(128)} %bitcast.pos_ref, bf16[1024,768]{1,0:T(8,128)(2,1)} %bitcast.25, bf16[1024,768]{1,0:T(8,128)(2,1)} %bitcast.26), custom_call_target="tpu_custom_call" | custom-call | tf_op jit(solution)/shard_map/pallas_call | solution.py:129
  63.5 0.0 copy-done.2
  63.5 9.0 %shard_map.38 = (f32[4,1,1024]{2,1,0:T(1,128)}, f32[4,1,1024]{2,1,0:T(1,128)}, f32[4,128,1024]{2,1,0:T(8,128)}) custom-call(s32[1]{0:T(128)} %bitcast.pos_ref, bf16[1024,768]{1,0:T(8,128)(2,1)} %bitcast.27, bf16[1024,256]{1,0:T(8,128)(2,1)} %copy-done.2), custom_call_target="tpu_custom_call" | custom-call | tf_op jit(solution)/shard_map/pallas_call | solution.py:129
  72.5 0.0 copy-done.4
  72.5 9.0 %shard_map.39 = (f32[4,1,1024]{2,1,0:T(1,128)}, f32[4,1,1024]{2,1,0:T(1,128)}, f32[4,128,1024]{2,1,0:T(8,128)}) custom-call(s32[1]{0:T(128)} %bitcast.pos_ref, bf16[1024,768]{1,0:T(8,128)(2,1)} %bitcast.28, bf16[1024,256]{1,0:T(8,128)(2,1)} %copy-done.4), custom_call_target="tpu_custom_call" | custom-call | tf_op jit(solution)/shard_map/pallas_call | solution.py:129
  81.6 0.0 collective-permute-done.2.kv_ref
  81.6 0.0 copy-start.3
  81.6 0.8 copy-done.3
  82.4 10.6 %shard_map.40 = bf16[1024,512]{1,0:T(8,128)(2,1)} custom-call(s32[1]{0:T(128)} %bitcast.pos_ref, bf16[1024,768]{1,0:T(8,128)(2,1)} %bitcast.29, bf16[1024,256]{1,0:T(8,128)(2,1)} %copy-done.3, f32[4,1,1024]{2,1,0:T(1,128)} %get-tuple-element.14.refs_0_, f32[4,1,1024]{2,1,0:T(1,128)} %get-tuple-element.15.refs_1_, f32[4,128,1024]{2,1,0:T(8,128)} %get-tuple-element.16.refs_2_, ...), custom_call_target="tpu_custom_call" | custom-call | tf_op jit(solution)/shard_map/pallas_call | solution.py:129
  93.0 16.4 %all_to_all.35 = bf16[8,128,512]{2,1,0:T(8,128)(2,1)S(1)} all-to-all(bf16[8,128,512]{2,1,0:T(8,128)(2,1)} %bitcast.30), channel_id=1, replica_groups=mesh['ctx'=32,'uly'=8] {'uly'}, dimensions={0} | all-to-all | bytes 2097152 | tf_op jit(solution)/shard_map/all_to_all | solution.py:154
  109.4 1.1 copy.11
  (1 shorter events, 0.0 us)
Async XLA Ops:
  0.0 1.4 %copy-start = (bf16[128,1024]{1,0:T(8,128)(2,1)S(1)}, bf16[128,1024]{1,0:T(8,128)(2,1)}, u32[]{:S(2)}) copy-start(bf16[128,1024]{1,0:T(8,128)(2,1)} %param.4) | copy-start | bytes 786436
  0.0 1.4 %copy-start.5 = (bf16[128,1024]{1,0:T(8,128)(2,1)S(1)}, bf16[128,1024]{1,0:T(8,128)(2,1)}, u32[]{:S(2)}) copy-start(bf16[128,1024]{1,0:T(8,128)(2,1)} %param.5) | copy-start | bytes 786436
  26.6 29.9 %copy-start.1 = (bf16[128,8,768]{2,0,1:T(8,128)(2,1)}, bf16[128,8,768]{2,0,1:T(8,128)(2,1)S(1)}, u32[]{:S(2)}) copy-start(bf16[128,8,768]{2,0,1:T(8,128)(2,1)S(1)} %all_to_all.34) | copy-start | bytes 4718596
  26.6 12.6 %collective-permute-start = (bf16[1024,256]{1,0:T(8,128)(2,1)S(1)}, bf16[1024,256]{1,0:T(8,128)(2,1)S(1)}, u32[]{:S(2)}, u32[]{:S(2)}) collective-permute-start(bf16[1024,256]{1,0:T(8,128)(2,1)S(1)} %slice.4), channel_id=1, source_target_pairs={{0,8},{8,16},{16,24},{24,32},{32,40},{40,48},{48,56},{56,64},{64,7... | collective-permute-start | bytes 1572872 | tf_op jit(solution)/shard_map/ppermute | solution.py:20
  39.2 24.3 %copy-start.2 = (bf16[1024,256]{1,0:T(8,128)(2,1)}, bf16[1024,256]{1,0:T(8,128)(2,1)S(1)}, u32[]{:S(2)}) copy-start(bf16[1024,256]{1,0:T(8,128)(2,1)S(1)} %collective-permute-done.kv_ref) | copy-start | bytes 1572868
  39.2 11.7 %collective-permute-start.1 = (bf16[1024,256]{1,0:T(8,128)(2,1)S(1)}, bf16[1024,256]{1,0:T(8,128)(2,1)S(1)}, u32[]{:S(2)}, u32[]{:S(2)}) collective-permute-start(bf16[1024,256]{1,0:T(8,128)(2,1)S(1)} %collective-permute-done.kv_ref), channel_id=1, source_target_pairs={{0,8},{8,16},{16,24},{24,32},{32,40},{40,48},{48,56},{56,64},{64,7... | collective-permute-start | bytes 1572872 | tf_op jit(solution)/shard_map/ppermute | solution.py:20
  50.9 21.6 %copy-start.4 = (bf16[1024,256]{1,0:T(8,128)(2,1)}, bf16[1024,256]{1,0:T(8,128)(2,1)S(1)}, u32[]{:S(2)}) copy-start(bf16[1024,256]{1,0:T(8,128)(2,1)S(1)} %collective-permute-done.1.kv_ref) | copy-start | bytes 1572868
  50.9 30.6 %collective-permute-start.2 = (bf16[1024,256]{1,0:T(8,128)(2,1)S(1)}, bf16[1024,256]{1,0:T(8,128)(2,1)S(1)}, u32[]{:S(2)}, u32[]{:S(2)}) collective-permute-start(bf16[1024,256]{1,0:T(8,128)(2,1)S(1)} %collective-permute-done.1.kv_ref), channel_id=1, source_target_pairs={{0,8},{8,16},{16,24},{24,32},{32,40},{40,48},{48,56},{56,64},{64,7... | collective-permute-start | bytes 1572872 | tf_op jit(solution)/shard_map/ppermute | solution.py:20
  81.6 0.8 copy-start.3
